TPU v7x, 256 devices: a whole 4x4x8 slice. The times are simulated.
256 devices in a mesh: row: 8 (over z), col: 32 (over y, x, core).
Axes of the slice: x: 4, y: 4, z: 8, core: 2. Of those that a mesh axis runs over, the one named last changes fastest.
Arguments:
- kernel: float32 [8, 8, 256, 2, 32, 256], P(None, 'row', None, None, 'col'), may hold values from 0 to 1.3, as said below
Outputs:
- factored: float32 [8, 8, 256, 2, 32, 256], P(None, 'row', None, None, 'col')
Inputs may be any that keep to these rules, and one draw needn't show every extreme that they name: kernel is symmetric and positive definite.
All inputs are finite; a program needn't handle non-finite values.
Results may differ from a plain program's by a relative error of at most 0.0003.
Values sent between devices are 32-bit elements; how exact they have to be, the bound alone decides.
No kernel may reach another device: no remote copies, remote signals or barrier semaphores. Data moves between devices by JAX's collectives and lax.ppermute only.
A program may use at most 64 MiB of HBM per device.

v0:
```python
import jax
import jax.numpy as jnp
from jax import lax
from jax.sharding import PartitionSpec as P


def from_root(block, axis, source):
    block = jnp.where(lax.axis_index(axis) == source, block, jnp.zeros_like(block))
    return lax.psum(block, axis)


def factor_panel(column, k, block_rows, row_count, col_count):
    tiles, width = (column.shape[0], column.shape[1])
    diag_raw = column[k // row_count]
    diag_block = from_root(diag_raw, "row", k % row_count)
    later = (block_rows > k)[:, None, None]
    same = (block_rows == k)[:, None, None]
    lower = jnp.linalg.cholesky(diag_block)
    flat = column.reshape(tiles * width, width)
    solved = jax.scipy.linalg.solve_triangular(lower, flat.T, lower=True).T.reshape(
        tiles, width, width
    )
    panel = jnp.where(later, solved, jnp.where(same, lower[None], 0.0))
    row_part = from_root(panel, "col", k % col_count)
    return (panel, row_part)


def column_part(row_part, my_col, row_count, col_count, col_tiles):
    wanted = (jnp.arange(col_tiles, dtype=jnp.int32) * col_count + my_col) // row_count
    chosen = jnp.take(row_part, wanted, axis=0)
    return from_root(chosen, "row", my_col % row_count)


def apply_update(work, k, panel, row_part, col_part, block_cols):
    product = jnp.einsum(
        "iab,jcb->iajc",
        row_part,
        col_part,
        precision=lax.Precision.HIGHEST,
        preferred_element_type=jnp.float32,
    )
    later = (block_cols > k)[None, None, :, None]
    same = (block_cols == k)[None, None, :, None]
    work = jnp.where(later, work - product, work)
    return jnp.where(same, panel[:, :, None, :], work)


def per_device(kernel):
    row_tiles, width, col_tiles = (kernel.shape[0], kernel.shape[2], kernel.shape[3])
    work = kernel.reshape(row_tiles, width, col_tiles, width)
    row_count = lax.axis_size("row")
    col_count = lax.axis_size("col")
    my_row = lax.axis_index("row")
    my_col = lax.axis_index("col")
    block_rows = jnp.arange(row_tiles, dtype=jnp.int32) * row_count + my_row
    block_cols = jnp.arange(col_tiles, dtype=jnp.int32) * col_count + my_col
    first_col = 0 // col_count
    next_col = 1 // col_count
    panel_zero, rows_zero = factor_panel(
        work[:, :, first_col, :], 0, block_rows, row_count, col_count
    )
    cols_zero = column_part(rows_zero, my_col, row_count, col_count, col_tiles)
    work = apply_update(work, 0, panel_zero, rows_zero, cols_zero, block_cols)
    panel_one, rows_one = factor_panel(work[:, :, next_col, :], 1, block_rows, row_count, col_count)
    cols_one = column_part(rows_one, my_col, row_count, col_count, col_tiles)
    work = apply_update(work, 1, panel_one, rows_one, cols_one, block_cols)
    upper = (block_rows < 2)[:, None, None, None] & (block_cols >= 2)[None, None, :, None]
    work = jnp.where(upper, 0.0, work)
    return work.reshape(row_tiles, 1, width, col_tiles, 1, width)


def solution(mesh):
    in_specs = (P(None, "row", None, None, "col", None),)
    out_specs = P(None, "row", None, None, "col", None)
    return jax.shard_map(
        per_device, mesh=mesh, in_specs=in_specs, out_specs=out_specs, check_vma=False
    )
```

profile of v0, /device:TPU:1, one launch (start us, length us, event | category | flops | bytes accessed | tf_op | source)
XLA Modules:
  0.0 729.8 jit_solution(3852850829479252524)
XLA Ops:
  6.5 10.9 %copy.12 = f32[8,1,256,2,1,256]{2,5,3,0,4,1:T(8,128)} copy(f32[8,1,256,2,1,256]{5,4,3,2,1,0:T(1,128)} %param.6) | data formatting | bytes 8388608 | tf_op args[0]
  17.4 1.7 fusion.13
  19.2 3.1 slice.71
  22.2 1.9 copy.14
  24.2 66.7 %all-reduce.8.cloned.1.call-done = f32[256,256]{0,1:T(8,128)} async-done(((f32[256,256]{0,1:T(8,128)}), f32[256,256]{0,1:T(8,128)}) %all-reduce.8.cloned.1.call-update) | async-done | bytes 262160 | tf_op jit(solution)/shard_map/psum | solution.py:9
  90.9 1.1 copy.13
  92.0 1.0 fusion.15
  93.0 11.7 %cholesky.130 = f32[128,128]{1,0:T(8,128)S(1)} custom-call(f32[128,128]{1,0:T(8,128)S(1)} %cholesky.194), custom_call_target="Cholesky" | custom-call | tf_op jit(solution)/shard_map/jit(cholesky)/cholesky | solution.py:18
  104.8 9.8 %custom-call.13 = f32[1,128,128]{1,2,0:T(8,128)S(1)} custom-call(f32[1,128,128]{2,1,0:T(8,128)S(1)} %get-tuple-element.59), custom_call_target="InvertDiagBlocksLowerTriangular" | custom-call | tf_op jit(solution)/shard_map/jit(cholesky)/cholesky | solution.py:18
  115.1 11.7 %cholesky.147 = f32[128,128]{1,0:T(8,128)S(1)} custom-call(f32[128,128]{1,0:T(8,128)S(1)} %convolution_subtract_fusion.3), custom_call_target="Cholesky" | custom-call | tf_op jit(solution)/shard_map/jit(cholesky)/cholesky | solution.py:18
  128.9 3.9 while.4
  129.5 1.3 bitcast_dynamic-update-slice_fusion.4
  131.5 1.3 bitcast_dynamic-update-slice_fusion.4
  132.8 20.1 %custom-call.14 = f32[2,128,128]{1,2,0:T(8,128)S(1)} custom-call(f32[2,128,128]{2,1,0:T(8,128)S(1)} %get-tuple-element.22), custom_call_target="InvertDiagBlocksLowerTriangular" | custom-call | tf_op jit(solution)/shard_map/jit(_solve_triangular)/triangular_solve | solution.py:20
  153.0 1.1 fusion.8
  154.0 1.8 convolution_subtract_fusion.1
  155.9 1.1 fusion.25
  157.1 1.9 copy.28
  159.0 3.4 broadcast_select_fusion.1
  162.5 121.1 %all-reduce.10.cloned.1.call-done = f32[8,256,256]{2,1,0:T(8,128)} async-done(((f32[8,256,256]{2,1,0:T(8,128)}), f32[8,256,256]{2,1,0:T(8,128)}) %all-reduce.10.cloned.1.call-update) | async-done | bytes 2097168 | tf_op jit(solution)/shard_map/psum | solution.py:9
  283.6 2.2 gather_fusion
  286.8 1.8 copy.16
  288.7 67.2 %all-reduce.12.cloned.1.call-done = f32[2,256,256]{2,1,0:T(8,128)} async-done(((f32[2,256,256]{2,1,0:T(8,128)}), f32[2,256,256]{2,1,0:T(8,128)}) %all-reduce.12.cloned.1.call-update) | async-done | bytes 524304 | tf_op jit(solution)/shard_map/psum | solution.py:9
  355.9 7.4 %fusion = f32[8,256,2,256]{1,3,2,0:T(8,128)S(1)} fusion(f32[8,256,256]{2,1,0:T(8,128)} %all-reduce.10.cloned.1.call-done, f32[8,256,256]{1,2,0:T(8,128)} %copy.16, pred[2]{0:T(512)(128)(4,1)S(1)} %get-tuple-element.64, pred[2]{0:T(512)(128)(4,1)S(1)} %get-tuple-element.65, f32[2,256,256]{2,1,0:T(8,128)} %all-reduce.12.cloned.1.call-done, ...), kind=kOutput, calls=%fused_computation.8 | convolution fusion | flops 3224371200 | bytes 13107204 | tf_op jit(solution)/shard_map/iab,jcb->iajc/dot_general | solution.py:35
  363.4 2.0 copy-done
  366.2 1.6 slice-done
  367.8 2.0 copy.19
  369.8 67.3 %all-reduce.14.cloned.1.call-done = f32[256,256]{0,1:T(8,128)} async-done(((f32[256,256]{0,1:T(8,128)}), f32[256,256]{0,1:T(8,128)}) %all-reduce.14.cloned.1.call-update) | async-done | bytes 262160 | tf_op jit(solution)/shard_map/psum | solution.py:9
  437.1 1.1 copy.18
  438.2 1.0 fusion.14
  439.2 11.7 %cholesky.164 = f32[128,128]{1,0:T(8,128)S(1)} custom-call(f32[128,128]{1,0:T(8,128)S(1)} %cholesky.197), custom_call_target="Cholesky" | custom-call | tf_op jit(solution)/shard_map/jit(cholesky)/cholesky | solution.py:18
  450.9 9.8 %custom-call.15 = f32[1,128,128]{1,2,0:T(8,128)S(1)} custom-call(f32[1,128,128]{2,1,0:T(8,128)S(1)} %get-tuple-element.55), custom_call_target="InvertDiagBlocksLowerTriangular" | custom-call | tf_op jit(solution)/shard_map/jit(cholesky)/cholesky | solution.py:18
  461.2 11.7 %cholesky.181 = f32[128,128]{1,0:T(8,128)S(1)} custom-call(f32[128,128]{1,0:T(8,128)S(1)} %convolution_subtract_fusion.2), custom_call_target="Cholesky" | custom-call | tf_op jit(solution)/shard_map/jit(cholesky)/cholesky | solution.py:18
  475.6 3.9 while.5
  476.2 1.3 bitcast_dynamic-update-slice_fusion.5
  478.1 1.3 bitcast_dynamic-update-slice_fusion.5
  479.5 19.9 %custom-call.16 = f32[2,128,128]{1,2,0:T(8,128)S(1)} custom-call(f32[2,128,128]{2,1,0:T(8,128)S(1)} %get-tuple-element.23), custom_call_target="InvertDiagBlocksLowerTriangular" | custom-call | tf_op jit(solution)/shard_map/jit(_solve_triangular)/triangular_solve | solution.py:20
  499.4 1.1 fusion.6
  500.5 1.8 convolution_subtract_fusion
  502.3 1.1 fusion.21
  503.5 1.8 copy.20
  505.3 3.5 broadcast_select_fusion
  508.9 121.2 %all-reduce.16.cloned.1.call-done = f32[8,256,256]{2,1,0:T(8,128)} async-done(((f32[8,256,256]{2,1,0:T(8,128)}), f32[8,256,256]{2,1,0:T(8,128)}) %all-reduce.16.cloned.1.call-update) | async-done | bytes 2097168 | tf_op jit(solution)/shard_map/psum | solution.py:9
  630.1 2.2 gather_fusion.1
  633.3 1.8 copy.21
  635.1 67.2 %all-reduce.18.cloned.1.call-done = f32[2,256,256]{2,1,0:T(8,128)} async-done(((f32[2,256,256]{2,1,0:T(8,128)}), f32[2,256,256]{2,1,0:T(8,128)}) %all-reduce.18.cloned.1.call-update) | async-done | bytes 524304 | tf_op jit(solution)/shard_map/psum | solution.py:9
  702.3 9.5 %fusion.3 = f32[8,1,256,2,1,256]{2,5,3,0,4,1:T(8,128)} fusion(f32[8,256,2,256]{1,3,2,0:T(8,128)} %copy-done, f32[8,256,256]{2,1,0:T(8,128)} %all-reduce.16.cloned.1.call-done, f32[8,256,256]{1,2,0:T(8,128)} %copy.21, pred[2]{0:T(512)(128)(4,1)S(1)} %get-tuple-element.66, pred[2]{0:T(512)(128)(4,1)S(1)} %get-tuple-element.67, ...), kind=kOutput, calls=%fused_computation.11 | convolution fusion | flops 3225419776 | bytes 13107220 | tf_op jit(solution)/shard_map/iab,jcb->iajc/dot_general | solution.py:35
  711.8 10.9 %copy.23 = f32[8,1,256,2,1,256]{5,4,3,2,1,0:T(1,128)} copy(f32[8,1,256,2,1,256]{2,5,3,0,4,1:T(8,128)} %fusion.3) | data formatting | bytes 8388608 | tf_op jit(solution)/shard_map/reshape | solution.py:69
  (60 shorter events, 9.2 us)
Async XLA Ops:
  6.5 84.4 %all-reduce.8.cloned.1.call-start = ((), (), s32[]{:S(2)}) async-start(), calls=%async_computation | async-start | bytes 524288 | tf_op jit(solution)/shard_map/psum | solution.py:9
  19.1 264.5 %all-reduce.10.cloned.1.call-start = ((), (), s32[]{:S(2)}) async-start(), calls=%async_computation.1 | async-start | bytes 4194304 | tf_op jit(solution)/shard_map/psum | solution.py:9
  162.4 193.5 %all-reduce.12.cloned.1.call-start = ((), (), s32[]{:S(2)}) async-start(), calls=%async_computation.2 | async-start | bytes 1048576 | tf_op jit(solution)/shard_map/psum | solution.py:9
  286.8 150.3 %all-reduce.14.cloned.1.call-start = ((), (), s32[]{:S(2)}) async-start(), calls=%async_computation.3 | async-start | bytes 524288 | tf_op jit(solution)/shard_map/psum | solution.py:9
  363.3 2.0 copy-start
  366.1 264.0 %all-reduce.16.cloned.1.call-start = ((), (), s32[]{:S(2)}) async-start(), calls=%async_computation.4 | async-start | bytes 4194304 | tf_op jit(solution)/shard_map/psum | solution.py:9
  366.2 1.6 slice-start
  369.8 129.6 %copy-start.1 = (f32[8,256,1,256]{3,1,0,2:T(8,128)S(1)}, f32[8,256,1,256]{3,1,0,2:T(8,128)}, u32[]{:S(2)}) copy-start(f32[8,256,1,256]{3,1,0,2:T(8,128)} %copy.19) | copy-start | bytes 6291460
  508.8 193.5 %all-reduce.18.cloned.1.call-start = ((), (), s32[]{:S(2)}) async-start(), calls=%async_computation.5 | async-start | bytes 1048576 | tf_op jit(solution)/shard_map/psum | solution.py:9
Sparse Core Ops, SparseCore 0:
  19.2 71.6 all-reduce.7
  162.5 121.0 all-reduce.9
  286.9 68.9 all-reduce.11
  366.2 70.7 all-reduce.13
  509.0 121.0 all-reduce.15
  633.3 68.9 all-reduce.17
where the time goes:
time: 743 us; the launch traced here: 730 us
  waiting for transfers between devices  511 us (69%)
  other arithmetic  122 us (16%)
  local copies, waits for them, and re-layouts  54.1 us (7%)
  matrix products  25.8 us (3%)
  between operations  16.5 us (2%)
    psum x6, waiting for transfers between devices, from_root(): return lax.psum(block, axis)  511 us
    another operation x13, other arithmetic, factor_panel(): lower = jnp.linalg.cholesky(diag_block)  68.6 us
    another operation x5, other arithmetic, factor_panel(): jax.scipy.linalg.solve_triangular(lower, flat.T, lower=True)  40.1 us
    dot_general x2, matrix products, apply_update(): jnp.einsum('iab,jcb->iajc', row_part, col_part, precision=lax.Precision.H...  17 us
  transfers between devices with their start and end apart: 6, of which 6 were waited for; matrix products, arithmetic and copies ran while one was open for 1% of the time, Pallas kernels for 0%

commit v1 on v0

v1 whole, which is shorter than its diff:
```python
import jax
import jax.numpy as jnp
from jax import lax
from jax.sharding import PartitionSpec as P

HIGH = lax.Precision.HIGHEST


def prescatter(pieces, axis, plan):
    me = lax.axis_index(axis)
    got = jnp.zeros_like(pieces[0])
    for q, pairs in enumerate(plan):
        moved = [(s, d) for s, d in pairs if s != d]
        kept = [s for s, d in pairs if s == d]
        if moved:
            got = got + lax.ppermute(pieces[q], axis, moved)
        for s in kept:
            got = got + jnp.where(me == s, pieces[q], jnp.zeros_like(pieces[q]))
    return got


def tri_solve(lower, rows):
    n, w = rows.shape[0], rows.shape[1]
    flat = rows.reshape(n * w, w)
    return jax.scipy.linalg.solve_triangular(lower, flat.T, lower=True).T.reshape(n, w, w)


def per_device(kernel):
    tiles, width, ucount = kernel.shape[0], kernel.shape[2], kernel.shape[3]
    work = kernel.reshape(tiles, width, ucount, width)
    nrow = lax.axis_size("row")
    ncol = lax.axis_size("col")
    my_row = lax.axis_index("row")
    my_col = lax.axis_index("col")
    half = width // 2

    rowblk = work[0]
    cpieces = [rowblk[(p % 2) * half:(p % 2 + 1) * half, p // 2, :] for p in range(2 * ucount)]
    d0 = [(-p) % nrow for p in range(2 * ucount)]
    d1 = [(1 + p) % nrow for p in range(2 * ucount)]
    cplan = [[(0, d0[p]), (1, d1[p])] for p in range(2 * ucount)]
    cmine = prescatter(cpieces, "row", cplan)
    cg = lax.all_gather(cmine, "row")

    def cblock(dest, u):
        return jnp.concatenate([cg[dest[2 * u]], cg[dest[2 * u + 1]]], axis=0)

    crow = [[cblock(d, u) for u in range(ucount)] for d in (d0, d1)]

    lead = jnp.concatenate([crow[0][0], crow[1][0]], axis=0)
    pcol = work[:, :, 0, :].reshape(tiles * width, width)
    npieces = ncol // 2
    rrows = pcol.shape[0] // npieces
    lrows = lead.shape[0] // npieces
    rplan = [[(0, 2 * q), (1, 2 * q + 1)] for q in range(npieces)]
    rmine = prescatter([pcol[q * rrows:(q + 1) * rrows] for q in range(npieces)], "col", rplan)
    lmine = prescatter([lead[q * lrows:(q + 1) * lrows] for q in range(npieces)], "col", rplan)
    rg = lax.all_gather(jnp.concatenate([rmine, lmine], axis=0), "col")

    def assemble(k):
        body = jnp.concatenate([rg[2 * q + k, :rrows] for q in range(npieces)], axis=0)
        tail = jnp.concatenate([rg[2 * q + k, rrows:] for q in range(npieces)], axis=0)
        return body.reshape(tiles, width, width), tail

    col0, lead0 = assemble(0)
    col1, lead1 = assemble(1)
    a00 = lead0[:width]
    a10 = lead0[width:]
    a11 = lead1[width:]

    block_rows = jnp.arange(tiles, dtype=jnp.int32) * nrow + my_row
    block_cols = jnp.arange(ucount, dtype=jnp.int32) * ncol + my_col
    cT0 = jnp.stack([crow[0][u].T for u in range(ucount)])
    cT1 = jnp.stack([crow[1][u].T for u in range(ucount)])

    g0 = jnp.linalg.cholesky(a00)
    x0 = tri_solve(g0, jnp.concatenate([col0, cT0, a10[None]], axis=0))
    x0r, x0c, x01 = x0[:tiles], x0[tiles:tiles + ucount], x0[tiles + ucount]
    a11u = a11 - jnp.dot(x01, x01.T, precision=HIGH, preferred_element_type=jnp.float32)
    g1 = jnp.linalg.cholesky(a11u)
    y1 = jnp.concatenate([col1, cT1], axis=0) - jnp.einsum(
        "nab,cb->nac", jnp.concatenate([x0r, x0c], axis=0), x01,
        precision=HIGH, preferred_element_type=jnp.float32)
    x1 = tri_solve(g1, y1)
    x1r, x1c = x1[:tiles], x1[tiles:]

    def mask(x, idx, k, g):
        later = (idx > k)[:, None, None]
        same = (idx == k)[:, None, None]
        return jnp.where(later, x, jnp.where(same, g[None], 0.0))

    p0r = mask(x0r, block_rows, 0, g0)
    p0c = mask(x0c, block_cols, 0, g0)
    p1r = mask(x1r, block_rows, 1, g1)
    p1c = mask(x1c, block_cols, 1, g1)

    def update(w, k, pr, pc):
        prod = jnp.einsum("iab,jcb->iajc", pr, pc, precision=HIGH,
                          preferred_element_type=jnp.float32)
        later = (block_cols > k)[None, None, :, None]
        same = (block_cols == k)[None, None, :, None]
        w = jnp.where(later, w - prod, w)
        return jnp.where(same, pr[:, :, None, :], w)

    work = update(work, 0, p0r, p0c)
    work = update(work, 1, p1r, p1c)
    upper = (block_rows < 2)[:, None, None, None] & (block_cols >= 2)[None, None, :, None]
    work = jnp.where(upper, 0.0, work)
    return work.reshape(tiles, 1, width, ucount, 1, width)


def solution(mesh):
    in_specs = (P(None, "row", None, None, "col", None),)
    out_specs = P(None, "row", None, None, "col", None)
    return jax.shard_map(
        per_device, mesh=mesh, in_specs=in_specs, out_specs=out_specs, check_vma=False
    )
```

time: 743 us -> 425 us (0.57)
  waiting for transfers between devices: 511 us -> 69.3 us
  starting transfers between devices: 0.21 us -> 69 us
  local copies, waits for them, and re-layouts: 54.1 us -> 105 us
    psum x6 -> x0, waiting for transfers between devices: 511 us -> none  [from_root(): return lax.psum(block, axis)]
    ppermute x0 -> x33, starting transfers between devices: none -> 68.9 us  [prescatter(): got = got + lax.ppermute(pieces[q], axis, moved)]
    all_gather x0 -> x2, waiting for transfers between devices: none -> 64.1 us  [the longest x1 49 us: per_device(): rg = lax.all_gather(jnp.concatenate([rmine, lmine], axis=0), 'col')]
    unnamed x5 -> x138, local copies, waits for them, and re-layouts: 12.9 us -> 51.2 us
    select_n x2 -> x8, local copies, waits for them, and re-layouts: 3.66 us -> 15.2 us  [the longest x6 14 us: mask(): return jnp.where(later, x, jnp.where(same, g[None], 0.0))]
    select_n x7 -> x3, other arithmetic: 11.1 us -> 3.44 us  [mask(): return jnp.where(later, x, jnp.where(same, g[None], 0.0))]
    another operation x18 -> x19, other arithmetic: 109 us -> 112 us  [the longest x5 42.2 us: tri_solve(): jax.scipy.linalg.solve_triangular(lower, flat.T, lower=True)]
    dot_general x2 -> x4, matrix products: 17 us -> 17.2 us  [the longest x2 11.9 us: update(): jnp.einsum('iab,jcb->iajc', pr, pc, precision=HIGH, preferred_element_typ...]
  transfers between devices with their start and end apart: 6 -> 35, of which waited for: 6 -> 4; matrix products, arithmetic and copies ran while one was open for 1% -> 4% of each run, Pallas kernels for 0% -> 0%
where the time goes in v1:
time: 425 us; the launch traced here: 419 us
  other arithmetic  128 us (30%)
  local copies, waits for them, and re-layouts  105 us (25%)
  waiting for transfers between devices  69.3 us (16%)
  starting transfers between devices  69 us (16%)
  matrix products  29.9 us (7%)
  between operations  17.3 us (4%)
    ppermute x33, starting transfers between devices, prescatter(): got = got + lax.ppermute(pieces[q], axis, moved)  68.9 us
    unnamed x138, local copies, waits for them, and re-layouts  51.2 us
    all_gather x1, waiting for transfers between devices, per_device(): rg = lax.all_gather(jnp.concatenate([rmine, lmine], axis=0), 'col')  49 us
    another operation x5, other arithmetic, tri_solve(): jax.scipy.linalg.solve_triangular(lower, flat.T, lower=True)  42.2 us
    another operation x7, other arithmetic, per_device(): g1 = jnp.linalg.cholesky(a11u)  34.9 us
    another operation x6, other arithmetic, per_device(): g0 = jnp.linalg.cholesky(a00)  34 us
    all_gather x1, waiting for transfers between devices, per_device(): cg = lax.all_gather(cmine, 'row')  15.1 us
    select_n x6, local copies, waits for them, and re-layouts, mask(): return jnp.where(later, x, jnp.where(same, g[None], 0.0))  14 us
  transfers between devices with their start and end apart: 35, of which 4 were waited for; matrix products, arithmetic and copies ran while one was open for 4% of the time, Pallas kernels for 0%

profile of v1, /device:TPU:1, one launch (start us, length us, event | category | flops | bytes accessed | tf_op | source)
XLA Modules:
  0.0 419.2 jit_solution(6551624672054431610)
XLA Ops:
  8.5 8.3 %collective-permute-start.15 = (f32[128,256]{0,1:T(8,128)S(1)}, f32[128,256]{0,1:T(8,128)S(1)}, u32[]{:S(2)}, u32[]{:S(2)}) collective-permute-start(f32[128,256]{0,1:T(8,128)S(1)} %get-tuple-element.136), channel_id=1, source_target_pairs={{0,224},{32,64},{1,225},{33,65},{2,226},{34,66},{3,227},{35,67},{4... | collective-permute-start | bytes 393224 | tf_op jit(solution)/shard_map/ppermute | solution.py:16
  19.4 2.3 collective-permute-done.16
  21.8 2.8 collective-permute-done.17
  25.3 2.7 copy.129
  29.2 3.1 collective-permute-start
  32.3 2.2 collective-permute-start.1
  34.5 3.0 collective-permute-start.10
  46.8 15.1 %all-gather.5.cloned.1.call-done = f32[1024,256]{0,1:T(8,128)} async-done(((f32[128,256]{0,1:T(8,128)}), f32[1024,256]{0,1:T(8,128)}) %all-gather.5.cloned.1.call-update) | async-done | bytes 1048592 | tf_op jit(solution)/shard_map/all_gather | solution.py:43
  61.8 2.5 copy.102
  64.4 7.1 %collective-permute-start.5 = (f32[128,256]{1,0:T(8,128)}, f32[128,256]{1,0:T(8,128)}, u32[]{:S(2)}, u32[]{:S(2)}) collective-permute-start(f32[128,256]{1,0:T(8,128)} %get-tuple-element.110), channel_id=1, source_target_pairs={{0,12},{1,13},{32,44},{33,45},{64,76},{65,77},{96,108},{97,109},{1... | collective-permute-start | bytes 393224 | tf_op jit(solution)/shard_map/ppermute | solution.py:16
  71.5 1.9 collective-permute-start.6
  73.4 1.9 collective-permute-start.7
  75.4 1.9 collective-permute-start.8
  77.3 1.9 collective-permute-start.9
  81.1 1.9 collective-permute-start.18
  83.0 1.9 collective-permute-start.19
  84.9 1.9 collective-permute-start.20
  86.8 1.9 collective-permute-start.21
  88.7 1.9 collective-permute-start.22
  92.5 1.9 collective-permute-start.24
  94.3 1.9 collective-permute-start.25
  96.2 1.9 collective-permute-start.26
  98.1 1.9 collective-permute-start.27
  117.4 49.0 %all-gather.7.cloned.1.call-done = f32[5120,256]{1,0:T(8,128)} async-done(((f32[160,256]{1,0:T(8,128)}), f32[5120,256]{1,0:T(8,128)}) %all-gather.7.cloned.1.call-update) | async-done | bytes 5242896 | tf_op jit(solution)/shard_map/all_gather | solution.py:58
  179.5 11.7 %cholesky.130 = f32[128,128]{1,0:T(8,128)S(1)} custom-call(f32[128,128]{1,0:T(8,128)S(1)} %cholesky.194), custom_call_target="Cholesky" | custom-call | tf_op jit(solution)/shard_map/jit(cholesky)/cholesky | solution.py:76
  191.3 9.8 %custom-call.19 = f32[1,128,128]{1,2,0:T(8,128)S(1)} custom-call(f32[1,128,128]{2,1,0:T(8,128)S(1)} %get-tuple-element.146), custom_call_target="InvertDiagBlocksLowerTriangular" | custom-call | tf_op jit(solution)/shard_map/jit(cholesky)/cholesky | solution.py:76
  201.6 11.7 %cholesky.147 = f32[128,128]{1,0:T(8,128)S(1)} custom-call(f32[128,128]{1,0:T(8,128)S(1)} %convolution_subtract_fusion.4), custom_call_target="Cholesky" | custom-call | tf_op jit(solution)/shard_map/jit(cholesky)/cholesky | solution.py:76
  216.8 4.1 while.2
  220.9 20.4 %custom-call.16 = f32[2,128,128]{1,2,0:T(8,128)} custom-call(f32[2,128,128]{2,1,0:T(8,128)S(1)} %get-tuple-element.13), custom_call_target="InvertDiagBlocksLowerTriangular" | custom-call | tf_op jit(solution)/shard_map/jit(_solve_triangular)/triangular_solve | solution.py:25
  275.5 2.7 pad_maximum_fusion
  279.6 2.5 convolution_subtract_fusion.1
  283.7 2.2 concatenate.47
  287.4 11.7 %cholesky.164 = f32[128,128]{1,0:T(8,128)S(1)} custom-call(f32[128,128]{1,0:T(8,128)S(1)} %cholesky.197), custom_call_target="Cholesky" | custom-call | tf_op jit(solution)/shard_map/jit(cholesky)/cholesky | solution.py:80
  299.2 10.0 %custom-call.20 = f32[1,128,128]{1,2,0:T(8,128)S(1)} custom-call(f32[1,128,128]{2,1,0:T(8,128)S(1)} %get-tuple-element.142), custom_call_target="InvertDiagBlocksLowerTriangular" | custom-call | tf_op jit(solution)/shard_map/jit(cholesky)/cholesky | solution.py:80
  311.3 11.7 %cholesky.181 = f32[128,128]{1,0:T(8,128)S(1)} custom-call(f32[128,128]{1,0:T(8,128)S(1)} %convolution_subtract_fusion.3), custom_call_target="Cholesky" | custom-call | tf_op jit(solution)/shard_map/jit(cholesky)/cholesky | solution.py:80
  326.6 4.1 while.3
  330.7 19.7 %custom-call.17 = f32[2,128,128]{1,2,0:T(8,128)S(1)} custom-call(f32[2,128,128]{2,1,0:T(8,128)S(1)} %get-tuple-element.21), custom_call_target="InvertDiagBlocksLowerTriangular" | custom-call | tf_op jit(solution)/shard_map/jit(_solve_triangular)/triangular_solve | solution.py:25
  353.5 2.0 copy.96
  361.0 2.3 copy.78
  363.3 4.7 %maximum_subtract_fusion = f32[10,256,256]{2,1,0:T(8,128)S(1)} fusion(f32[1,256,256]{2,1,0:T(8,128)S(1)} %copy-done.11, f32[1,256,256]{2,1,0:T(8,128)S(1)} %copy-done.10, f32[8,256,256]{2,1,0:T(8,128)} %bitcast.441, f32[2,256,256]{2,1,0:T(8,128)S(1)} %bitcast.445, f32[8,256,256]{2,1,0:T(8,128)} %copy.78, f32[2816,256]{0,1:T(8,128)} %copy-done.1), kind=kOutput, calls=%fused_computation.15 | convolution fusion | flops 2015887360 | bytes 8126464 | tf_op jit(solution)/shard_map/nab,cb->nac/dot_general | solution.py:81
  369.3 2.3 convolution_subtract_fusion
  379.4 3.0 copy.82
  382.3 2.9 copy.84
  386.6 3.0 copy.100
  390.5 3.2 copy.98
  393.8 5.5 %fusion.92 = f32[8,256,2,256]{3,1,2,0:T(8,128)S(1)} fusion(f32[8,256,256,1]{2,1,3,0:T(8,128)} %bitcast.409, f32[2,256,256,1]{2,1,0,3:T(8,128)S(1)} %bitcast.453), kind=kOutput, calls=%fused_computation.223 | convolution fusion | flops 3221225472 | bytes 6815744 | tf_op jit(solution)/shard_map/iab,jcb->iajc/dot_general | solution.py:98
  399.4 6.4 %fusion.3 = f32[8,1,256,2,1,256]{5,2,3,0,4,1:T(8,128)S(1)} fusion(f32[8,256,2,256]{3,1,2,0:T(8,128)S(1)} %fusion.92, f32[8,256,256,1]{2,1,3,0:T(8,128)} %bitcast.406, f32[2,256,256,1]{2,1,0,3:T(8,128)S(1)} %bitcast.446, f32[8,256,256]{2,1,0:T(8,128)S(1)} %copy-done.3, f32[8,256,256]{2,1,0:T(8,128)S(1)} %copy-done.2, pred[2]{0:T(512)(128)(4,1)S(1)} %copy-done.34, ...), kind=kOutput, calls=%fused_computation.9 | convolution fusion | flops 3228565504 | bytes 19398680 | tf_op jit(solution)/shard_map/iab,jcb->iajc/dot_general | solution.py:98
  405.8 6.3 %copy.91 = f32[8,1,256,2,1,256]{5,4,3,2,1,0:T(1,128)} copy(f32[8,1,256,2,1,256]{5,2,3,0,4,1:T(8,128)S(1)} %fusion.3) | data formatting | bytes 8388608 | tf_op jit(solution)/shard_map/reshape | solution.py:109
  (282 shorter events, 123.3 us)
Async XLA Ops:
  6.5 55.3 %all-gather.5.cloned.1.call-start = ((), (), s32[]{:S(2)}) async-start(), calls=%async_computation | async-start | bytes 1179648 | tf_op jit(solution)/shard_map/all_gather | solution.py:43
  8.5 10.9 %collective-permute-start.15 = (f32[128,256]{0,1:T(8,128)S(1)}, f32[128,256]{0,1:T(8,128)S(1)}, u32[]{:S(2)}, u32[]{:S(2)}) collective-permute-start(f32[128,256]{0,1:T(8,128)S(1)} %get-tuple-element.136), channel_id=1, source_target_pairs={{0,224},{32,64},{1,225},{33,65},{2,226},{34,66},{3,227},{35,67},{4... | collective-permute-start | bytes 393224 | tf_op jit(solution)/shard_map/ppermute | solution.py:16
  16.8 5.0 %collective-permute-start.16 = (f32[128,256]{0,1:T(8,128)S(1)}, f32[128,256]{0,1:T(8,128)S(1)}, u32[]{:S(2)}, u32[]{:S(2)}) collective-permute-start(f32[128,256]{0,1:T(8,128)S(1)} %get-tuple-element.138), channel_id=1, source_target_pairs={{0,192},{32,96},{1,193},{33,97},{2,194},{34,98},{3,195},{35,99},{4... | collective-permute-start | bytes 393224 | tf_op jit(solution)/shard_map/ppermute | solution.py:16
  18.1 6.5 %collective-permute-start.17 = (f32[128,256]{0,1:T(8,128)S(1)}, f32[128,256]{0,1:T(8,128)S(1)}, u32[]{:S(2)}, u32[]{:S(2)}) collective-permute-start(f32[128,256]{0,1:T(8,128)S(1)} %get-tuple-element.137), channel_id=1, source_target_pairs={{0,160},{32,128},{1,161},{33,129},{2,162},{34,130},{3,163},{35,131... | collective-permute-start | bytes 393224 | tf_op jit(solution)/shard_map/ppermute | solution.py:16
  25.3 141.2 %all-gather.7.cloned.1.call-start = ((), (), s32[]{:S(2)}) async-start(), calls=%async_computation.1 | async-start | bytes 5406720 | tf_op jit(solution)/shard_map/all_gather | solution.py:58
  29.2 11.0 %collective-permute-start = (f32[128,256]{1,0:T(8,128)S(1)}, f32[128,256]{1,0:T(8,128)S(1)}, u32[]{:S(2)}, u32[]{:S(2)}) collective-permute-start(f32[128,256]{1,0:T(8,128)S(1)} %get-tuple-element.100), channel_id=1, source_target_pairs={{0,2},{1,3},{32,34},{33,35},{64,66},{65,67},{96,98},{97,99},{128,1... | collective-permute-start | bytes 393224 | tf_op jit(solution)/shard_map/ppermute | solution.py:16
  32.3 9.2 %collective-permute-start.1 = (f32[128,256]{1,0:T(8,128)S(1)}, f32[128,256]{1,0:T(8,128)S(1)}, u32[]{:S(2)}, u32[]{:S(2)}) collective-permute-start(f32[128,256]{1,0:T(8,128)S(1)} %get-tuple-element.114), channel_id=1, source_target_pairs={{0,4},{1,5},{32,36},{33,37},{64,68},{65,69},{96,100},{97,101},{128... | collective-permute-start | bytes 393224 | tf_op jit(solution)/shard_map/ppermute | solution.py:16
  34.5 8.3 %collective-permute-start.10 = (f32[128,256]{1,0:T(8,128)S(1)}, f32[128,256]{1,0:T(8,128)S(1)}, u32[]{:S(2)}, u32[]{:S(2)}) collective-permute-start(f32[128,256]{1,0:T(8,128)S(1)} %get-tuple-element.105), channel_id=1, source_target_pairs={{0,22},{1,23},{32,54},{33,55},{64,86},{65,87},{96,118},{97,119},{1... | collective-permute-start | bytes 393224 | tf_op jit(solution)/shard_map/ppermute | solution.py:16
  37.6 6.6 %collective-permute-start.11 = (f32[128,256]{1,0:T(8,128)S(1)}, f32[128,256]{1,0:T(8,128)S(1)}, u32[]{:S(2)}, u32[]{:S(2)}) collective-permute-start(f32[128,256]{1,0:T(8,128)S(1)} %get-tuple-element.104), channel_id=1, source_target_pairs={{0,24},{1,25},{32,56},{33,57},{64,88},{65,89},{96,120},{97,121},{1... | collective-permute-start | bytes 393224 | tf_op jit(solution)/shard_map/ppermute | solution.py:16
  38.9 6.6 %collective-permute-start.12 = (f32[128,256]{1,0:T(8,128)S(1)}, f32[128,256]{1,0:T(8,128)S(1)}, u32[]{:S(2)}, u32[]{:S(2)}) collective-permute-start(f32[128,256]{1,0:T(8,128)S(1)} %get-tuple-element.103), channel_id=1, source_target_pairs={{0,26},{1,27},{32,58},{33,59},{64,90},{65,91},{96,122},{97,123},{1... | collective-permute-start | bytes 393224 | tf_op jit(solution)/shard_map/ppermute | solution.py:16
  40.2 24.2 %collective-permute-start.13 = (f32[128,256]{1,0:T(8,128)}, f32[128,256]{1,0:T(8,128)S(1)}, u32[]{:S(2)}, u32[]{:S(2)}) collective-permute-start(f32[128,256]{1,0:T(8,128)} %get-tuple-element.102), channel_id=1, source_target_pairs={{0,28},{1,29},{32,60},{33,61},{64,92},{65,93},{96,124},{97,125},{1... | collective-permute-start | bytes 393224 | tf_op jit(solution)/shard_map/ppermute | solution.py:16
  41.5 30.0 %collective-permute-start.14 = (f32[128,256]{1,0:T(8,128)}, f32[128,256]{1,0:T(8,128)S(1)}, u32[]{:S(2)}, u32[]{:S(2)}) collective-permute-start(f32[128,256]{1,0:T(8,128)} %get-tuple-element.101), channel_id=1, source_target_pairs={{0,30},{1,31},{32,62},{33,63},{64,94},{65,95},{96,126},{97,127},{1... | collective-permute-start | bytes 393224 | tf_op jit(solution)/shard_map/ppermute | solution.py:16
  42.8 30.6 %collective-permute-start.2 = (f32[128,256]{1,0:T(8,128)}, f32[128,256]{1,0:T(8,128)S(1)}, u32[]{:S(2)}, u32[]{:S(2)}) collective-permute-start(f32[128,256]{1,0:T(8,128)} %get-tuple-element.113), channel_id=1, source_target_pairs={{0,6},{1,7},{32,38},{33,39},{64,70},{65,71},{96,102},{97,103},{128... | collective-permute-start | bytes 393224 | tf_op jit(solution)/shard_map/ppermute | solution.py:16
  44.1 35.1 %copy-start.16 = (f32[128,256]{1,0:T(8,128)}, f32[128,256]{1,0:T(8,128)S(1)}, u32[]{:S(2)}) copy-start(f32[128,256]{1,0:T(8,128)S(1)} %collective-permute-done.11) | copy-start | bytes 393220
  44.1 31.2 %collective-permute-start.3 = (f32[128,256]{1,0:T(8,128)}, f32[128,256]{1,0:T(8,128)S(1)}, u32[]{:S(2)}, u32[]{:S(2)}) collective-permute-start(f32[128,256]{1,0:T(8,128)} %get-tuple-element.112), channel_id=1, source_target_pairs={{0,8},{1,9},{32,40},{33,41},{64,72},{65,73},{96,104},{97,105},{128... | collective-permute-start | bytes 393224 | tf_op jit(solution)/shard_map/ppermute | solution.py:16
  45.5 33.8 %copy-start.17 = (f32[128,256]{1,0:T(8,128)}, f32[128,256]{1,0:T(8,128)S(1)}, u32[]{:S(2)}) copy-start(f32[128,256]{1,0:T(8,128)S(1)} %collective-permute-done.12) | copy-start | bytes 393220
  45.5 31.8 %collective-permute-start.4 = (f32[128,256]{1,0:T(8,128)S(1)}, f32[128,256]{1,0:T(8,128)S(1)}, u32[]{:S(2)}, u32[]{:S(2)}) collective-permute-start(f32[128,256]{1,0:T(8,128)S(1)} %get-tuple-element.111), channel_id=1, source_target_pairs={{0,10},{1,11},{32,42},{33,43},{64,74},{65,75},{96,106},{97,107},{1... | collective-permute-start | bytes 393224 | tf_op jit(solution)/shard_map/ppermute | solution.py:16
  64.4 14.9 %copy-start.18 = (f32[128,256]{1,0:T(8,128)}, f32[128,256]{1,0:T(8,128)S(1)}, u32[]{:S(2)}) copy-start(f32[128,256]{1,0:T(8,128)S(1)} %collective-permute-done.13) | copy-start | bytes 393220
  64.4 16.7 %collective-permute-start.5 = (f32[128,256]{1,0:T(8,128)}, f32[128,256]{1,0:T(8,128)}, u32[]{:S(2)}, u32[]{:S(2)}) collective-permute-start(f32[128,256]{1,0:T(8,128)} %get-tuple-element.110), channel_id=1, source_target_pairs={{0,12},{1,13},{32,44},{33,45},{64,76},{65,77},{96,108},{97,109},{1... | collective-permute-start | bytes 393224 | tf_op jit(solution)/shard_map/ppermute | solution.py:16
  71.5 7.8 %copy-start.19 = (f32[128,256]{1,0:T(8,128)}, f32[128,256]{1,0:T(8,128)S(1)}, u32[]{:S(2)}) copy-start(f32[128,256]{1,0:T(8,128)S(1)} %collective-permute-done.14) | copy-start | bytes 393220
  71.5 11.5 %collective-permute-start.6 = (f32[128,256]{1,0:T(8,128)}, f32[128,256]{1,0:T(8,128)}, u32[]{:S(2)}, u32[]{:S(2)}) collective-permute-start(f32[128,256]{1,0:T(8,128)} %get-tuple-element.109), channel_id=1, source_target_pairs={{0,14},{1,15},{32,46},{33,47},{64,78},{65,79},{96,110},{97,111},{1... | collective-permute-start | bytes 393224 | tf_op jit(solution)/shard_map/ppermute | solution.py:16
  73.4 11.5 %collective-permute-start.7 = (f32[128,256]{1,0:T(8,128)}, f32[128,256]{1,0:T(8,128)}, u32[]{:S(2)}, u32[]{:S(2)}) collective-permute-start(f32[128,256]{1,0:T(8,128)} %get-tuple-element.108), channel_id=1, source_target_pairs={{0,16},{1,17},{32,48},{33,49},{64,80},{65,81},{96,112},{97,113},{1... | collective-permute-start | bytes 393224 | tf_op jit(solution)/shard_map/ppermute | solution.py:16
  75.4 11.4 %collective-permute-start.8 = (f32[128,256]{1,0:T(8,128)}, f32[128,256]{1,0:T(8,128)}, u32[]{:S(2)}, u32[]{:S(2)}) collective-permute-start(f32[128,256]{1,0:T(8,128)} %get-tuple-element.107), channel_id=1, source_target_pairs={{0,18},{1,19},{32,50},{33,51},{64,82},{65,83},{96,114},{97,115},{1... | collective-permute-start | bytes 393224 | tf_op jit(solution)/shard_map/ppermute | solution.py:16
  77.3 11.4 %collective-permute-start.9 = (f32[128,256]{1,0:T(8,128)}, f32[128,256]{1,0:T(8,128)}, u32[]{:S(2)}, u32[]{:S(2)}) collective-permute-start(f32[128,256]{1,0:T(8,128)} %get-tuple-element.106), channel_id=1, source_target_pairs={{0,20},{1,21},{32,52},{33,53},{64,84},{65,85},{96,116},{97,117},{1... | collective-permute-start | bytes 393224 | tf_op jit(solution)/shard_map/ppermute | solution.py:16
  79.3 36.5 %copy-start.4 = (f32[1024,256]{0,1:T(8,128)S(1)}, f32[1024,256]{0,1:T(8,128)}, u32[]{:S(2)}) copy-start(f32[1024,256]{0,1:T(8,128)} %all-gather.5.cloned.1.call-done) | copy-start | bytes 3145732
  81.1 9.5 %collective-permute-start.18 = (f32[32,256]{1,0:T(8,128)S(1)}, f32[32,256]{1,0:T(8,128)}, u32[]{:S(2)}, u32[]{:S(2)}) collective-permute-start(f32[32,256]{1,0:T(8,128)S(1)} %get-tuple-element.121), channel_id=1, source_target_pairs={{0,2},{1,3},{32,34},{33,35},{64,66},{65,67},{96,98},{97,99},{128,1... | collective-permute-start | bytes 98312 | tf_op jit(solution)/shard_map/ppermute | solution.py:16
  83.0 9.5 %collective-permute-start.19 = (f32[32,256]{1,0:T(8,128)S(1)}, f32[32,256]{1,0:T(8,128)}, u32[]{:S(2)}, u32[]{:S(2)}) collective-permute-start(f32[32,256]{1,0:T(8,128)S(1)} %get-tuple-element.135), channel_id=1, source_target_pairs={{0,4},{1,5},{32,36},{33,37},{64,68},{65,69},{96,100},{97,101},{128... | collective-permute-start | bytes 98312 | tf_op jit(solution)/shard_map/ppermute | solution.py:16
  84.9 9.4 %collective-permute-start.20 = (f32[32,256]{1,0:T(8,128)S(1)}, f32[32,256]{1,0:T(8,128)}, u32[]{:S(2)}, u32[]{:S(2)}) collective-permute-start(f32[32,256]{1,0:T(8,128)S(1)} %get-tuple-element.134), channel_id=1, source_target_pairs={{0,6},{1,7},{32,38},{33,39},{64,70},{65,71},{96,102},{97,103},{128... | collective-permute-start | bytes 98312 | tf_op jit(solution)/shard_map/ppermute | solution.py:16
  86.8 9.4 %collective-permute-start.21 = (f32[32,256]{1,0:T(8,128)S(1)}, f32[32,256]{1,0:T(8,128)}, u32[]{:S(2)}, u32[]{:S(2)}) collective-permute-start(f32[32,256]{1,0:T(8,128)S(1)} %get-tuple-element.133), channel_id=1, source_target_pairs={{0,8},{1,9},{32,40},{33,41},{64,72},{65,73},{96,104},{97,105},{128... | collective-permute-start | bytes 98312 | tf_op jit(solution)/shard_map/ppermute | solution.py:16
  88.7 9.4 %collective-permute-start.22 = (f32[32,256]{1,0:T(8,128)S(1)}, f32[32,256]{1,0:T(8,128)}, u32[]{:S(2)}, u32[]{:S(2)}) collective-permute-start(f32[32,256]{1,0:T(8,128)S(1)} %get-tuple-element.132), channel_id=1, source_target_pairs={{0,10},{1,11},{32,42},{33,43},{64,74},{65,75},{96,106},{97,107},{1... | collective-permute-start | bytes 98312 | tf_op jit(solution)/shard_map/ppermute | solution.py:16
  90.6 9.4 %collective-permute-start.23 = (f32[32,256]{1,0:T(8,128)}, f32[32,256]{1,0:T(8,128)}, u32[]{:S(2)}, u32[]{:S(2)}) collective-permute-start(f32[32,256]{1,0:T(8,128)} %get-tuple-element.131), channel_id=1, source_target_pairs={{0,12},{1,13},{32,44},{33,45},{64,76},{65,77},{96,108},{97,109},{1... | collective-permute-start | bytes 98312 | tf_op jit(solution)/shard_map/ppermute | solution.py:16
  92.5 8.8 %collective-permute-start.24 = (f32[32,256]{1,0:T(8,128)}, f32[32,256]{1,0:T(8,128)}, u32[]{:S(2)}, u32[]{:S(2)}) collective-permute-start(f32[32,256]{1,0:T(8,128)} %get-tuple-element.130), channel_id=1, source_target_pairs={{0,14},{1,15},{32,46},{33,47},{64,78},{65,79},{96,110},{97,111},{1... | collective-permute-start | bytes 98312 | tf_op jit(solution)/shard_map/ppermute | solution.py:16
  94.3 8.3 %collective-permute-start.25 = (f32[32,256]{1,0:T(8,128)}, f32[32,256]{1,0:T(8,128)}, u32[]{:S(2)}, u32[]{:S(2)}) collective-permute-start(f32[32,256]{1,0:T(8,128)} %get-tuple-element.129), channel_id=1, source_target_pairs={{0,16},{1,17},{32,48},{33,49},{64,80},{65,81},{96,112},{97,113},{1... | collective-permute-start | bytes 98312 | tf_op jit(solution)/shard_map/ppermute | solution.py:16
  96.2 7.7 %collective-permute-start.26 = (f32[32,256]{1,0:T(8,128)}, f32[32,256]{1,0:T(8,128)}, u32[]{:S(2)}, u32[]{:S(2)}) collective-permute-start(f32[32,256]{1,0:T(8,128)} %get-tuple-element.128), channel_id=1, source_target_pairs={{0,18},{1,19},{32,50},{33,51},{64,82},{65,83},{96,114},{97,115},{1... | collective-permute-start | bytes 98312 | tf_op jit(solution)/shard_map/ppermute | solution.py:16
  98.1 7.1 %collective-permute-start.27 = (f32[32,256]{1,0:T(8,128)}, f32[32,256]{1,0:T(8,128)}, u32[]{:S(2)}, u32[]{:S(2)}) collective-permute-start(f32[32,256]{1,0:T(8,128)} %get-tuple-element.127), channel_id=1, source_target_pairs={{0,20},{1,21},{32,52},{33,53},{64,84},{65,85},{96,116},{97,117},{1... | collective-permute-start | bytes 98312 | tf_op jit(solution)/shard_map/ppermute | solution.py:16
  100.0 8.6 %collective-permute-start.28 = (f32[32,256]{1,0:T(8,128)}, f32[32,256]{1,0:T(8,128)S(1)}, u32[]{:S(2)}, u32[]{:S(2)}) collective-permute-start(f32[32,256]{1,0:T(8,128)} %get-tuple-element.126), channel_id=1, source_target_pairs={{0,22},{1,23},{32,54},{33,55},{64,86},{65,87},{96,118},{97,119},{1... | collective-permute-start | bytes 98312 | tf_op jit(solution)/shard_map/ppermute | solution.py:16
  101.3 7.3 %collective-permute-start.29 = (f32[32,256]{1,0:T(8,128)}, f32[32,256]{1,0:T(8,128)S(1)}, u32[]{:S(2)}, u32[]{:S(2)}) collective-permute-start(f32[32,256]{1,0:T(8,128)} %get-tuple-element.125), channel_id=1, source_target_pairs={{0,24},{1,25},{32,56},{33,57},{64,88},{65,89},{96,120},{97,121},{1... | collective-permute-start | bytes 98312 | tf_op jit(solution)/shard_map/ppermute | solution.py:16
  102.6 6.0 %collective-permute-start.30 = (f32[32,256]{1,0:T(8,128)}, f32[32,256]{1,0:T(8,128)S(1)}, u32[]{:S(2)}, u32[]{:S(2)}) collective-permute-start(f32[32,256]{1,0:T(8,128)} %get-tuple-element.124), channel_id=1, source_target_pairs={{0,26},{1,27},{32,58},{33,59},{64,90},{65,91},{96,122},{97,123},{1... | collective-permute-start | bytes 98312 | tf_op jit(solution)/shard_map/ppermute | solution.py:16
  103.9 4.7 %collective-permute-start.31 = (f32[32,256]{1,0:T(8,128)}, f32[32,256]{1,0:T(8,128)S(1)}, u32[]{:S(2)}, u32[]{:S(2)}) collective-permute-start(f32[32,256]{1,0:T(8,128)} %get-tuple-element.123), channel_id=1, source_target_pairs={{0,28},{1,29},{32,60},{33,61},{64,92},{65,93},{96,124},{97,125},{1... | collective-permute-start | bytes 98312 | tf_op jit(solution)/shard_map/ppermute | solution.py:16
  105.2 3.4 collective-permute-start.32
  112.2 54.3 %copy-start.31 = (pred[8]{0:T(512)(128)(4,1)}, pred[8]{0:T(512)(128)(4,1)S(1)}, u32[]{:S(2)}) copy-start(pred[8]{0:T(512)(128)(4,1)S(1)} %get-tuple-element.152) | copy-start | bytes 28
  113.3 53.1 %copy-start.39 = (pred[2]{0:T(512)(128)(4,1)}, pred[2]{0:T(512)(128)(4,1)S(1)}, u32[]{:S(2)}) copy-start(pred[2]{0:T(512)(128)(4,1)S(1)} %get-tuple-element.158) | copy-start | bytes 10
  220.9 41.5 %copy-start.43 = (s32[2,2]{1,0:T(2,128)}, s32[2,2]{1,0:T(2,128)S(1)}, u32[]{:S(2)}) copy-start(s32[2,2]{1,0:T(2,128)S(1)} %get-tuple-element.298) | copy-start | bytes 52
  262.3 13.2 %copy-start.12 = (f32[1,256,256]{2,1,0:T(8,128)S(1)}, f32[1,256,256]{2,1,0:T(8,128)}, u32[]{:S(2)}) copy-start(f32[1,256,256]{2,1,0:T(8,128)} %get-tuple-element.160) | copy-start | bytes 786436
  262.3 13.2 %copy-start.15 = (f32[256,256]{1,0:T(8,128)S(1)}, f32[256,256]{1,0:T(8,128)}, u32[]{:S(2)}) copy-start(f32[256,256]{1,0:T(8,128)} %constant_dynamic-update-slice_fusion) | copy-start | bytes 786436
  283.7 72.8 %copy-start.1 = (f32[2816,256]{0,1:T(8,128)}, f32[2816,256]{0,1:T(8,128)S(1)}, u32[]{:S(2)}) copy-start(f32[2816,256]{0,1:T(8,128)S(1)} %maximum_bitcast_fusion) | copy-start | bytes 8650756
  285.9 40.7 %copy-start.44 = (s32[2,2]{1,0:T(2,128)S(1)}, s32[2,2]{1,0:T(2,128)}, u32[]{:S(2)}) copy-start(s32[2,2]{1,0:T(2,128)} %copy-done.43) | copy-start | bytes 52
  390.5 8.8 %copy-start.3 = (f32[8,256,256]{2,1,0:T(8,128)S(1)}, f32[8,256,256]{2,1,0:T(8,128)}, u32[]{:S(2)}) copy-start(f32[8,256,256]{2,1,0:T(8,128)} %copy.84) | copy-start | bytes 6291460
  (32 other events, 95.8 us)
Sparse Core Ops, SparseCore 0:
  25.4 36.3 all-gather.4
  110.4 55.9 all-gather.6

commit v2 on v1

v2 whole, which is shorter than its diff:
```python
import jax
import jax.numpy as jnp
from jax import lax
from jax.sharding import PartitionSpec as P

HIGH = lax.Precision.HIGHEST


def prescatter(pieces, axis, plan):
    me = lax.axis_index(axis)
    got = jnp.zeros_like(pieces[0])
    for q, pairs in enumerate(plan):
        moved = [(s, d) for s, d in pairs if s != d]
        kept = [s for s, d in pairs if s == d]
        if moved:
            got = got + lax.ppermute(pieces[q], axis, moved)
        for s in kept:
            got = got + jnp.where(me == s, pieces[q], jnp.zeros_like(pieces[q]))
    return got


def per_device(kernel):
    tiles, width, ucount = kernel.shape[0], kernel.shape[2], kernel.shape[3]
    work = kernel.reshape(tiles, width, ucount, width)
    nrow = lax.axis_size("row")
    ncol = lax.axis_size("col")
    my_row = lax.axis_index("row")
    my_col = lax.axis_index("col")
    half = width // 2

    rowblk = work[0]
    cpieces = [rowblk[(p % 2) * half:(p % 2 + 1) * half, p // 2, :] for p in range(2 * ucount)]
    d0 = [(-p) % nrow for p in range(2 * ucount)]
    d1 = [(1 + p) % nrow for p in range(2 * ucount)]
    cplan = [[(0, d0[p]), (1, d1[p])] for p in range(2 * ucount)]
    cmine = prescatter(cpieces, "row", cplan)
    cg = lax.all_gather(cmine, "row")

    def cblock(dest, u):
        return jnp.concatenate([cg[dest[2 * u]], cg[dest[2 * u + 1]]], axis=0)

    crow = [[cblock(d, u) for u in range(ucount)] for d in (d0, d1)]

    blk = work[0, :, 0, :]
    shifts = list(range(1, nrow))
    recv = jnp.stack([lax.ppermute(blk, "row", [(0, s), (1, (1 + s) % nrow)]) for s in shifts])
    from0 = lax.dynamic_index_in_dim(recv, jnp.maximum(my_row - 1, 0), keepdims=False)
    from1 = lax.dynamic_index_in_dim(recv, (my_row + nrow - 2) % nrow, keepdims=False)
    a0c = jnp.where(my_row == 0, blk, from0)
    a1c = jnp.where(my_row == 1, blk, from1)
    lead = jnp.concatenate([a0c, a1c], axis=0)
    pcol = work[:, :, 0, :].reshape(tiles * width, width)
    npieces = ncol // 2
    rrows = pcol.shape[0] // npieces
    lrows = lead.shape[0] // npieces
    rplan = [[(0, 2 * q), (1, 2 * q + 1)] for q in range(npieces)]
    rmine = prescatter([pcol[q * rrows:(q + 1) * rrows] for q in range(npieces)], "col", rplan)
    lmine = prescatter([lead[q * lrows:(q + 1) * lrows] for q in range(npieces)], "col", rplan)
    rg = lax.all_gather(jnp.concatenate([rmine, lmine], axis=0), "col")
    rg = rg.reshape(npieces, 2, rrows + lrows, width)

    col0 = rg[:, 0, :rrows].reshape(tiles, width, width)
    col1 = rg[:, 1, :rrows].reshape(tiles, width, width)
    lead0 = rg[:, 0, rrows:].reshape(2 * width, width)
    lead1 = rg[:, 1, rrows:].reshape(2 * width, width)
    a00 = lead0[:width]
    a10 = lead0[width:]
    a11 = lead1[width:]

    block_rows = jnp.arange(tiles, dtype=jnp.int32) * nrow + my_row
    block_cols = jnp.arange(ucount, dtype=jnp.int32) * ncol + my_col
    cT0 = jnp.stack([crow[0][u].T for u in range(ucount)])
    cT1 = jnp.stack([crow[1][u].T for u in range(ucount)])
    eye = jnp.eye(width, dtype=jnp.float32)

    def times_inv_t(y, ginv):
        return jnp.einsum("nab,cb->nac", y, ginv, precision=HIGH,
                          preferred_element_type=jnp.float32)

    g0 = jnp.linalg.cholesky(a00)
    g0i = jax.scipy.linalg.solve_triangular(g0, eye, lower=True)
    x0 = times_inv_t(jnp.concatenate([col0, cT0, a10[None]], axis=0), g0i)
    x0r, x0c, x01 = x0[:tiles], x0[tiles:tiles + ucount], x0[tiles + ucount]
    a11u = a11 - jnp.dot(x01, x01.T, precision=HIGH, preferred_element_type=jnp.float32)
    g1 = jnp.linalg.cholesky(a11u)
    g1i = jax.scipy.linalg.solve_triangular(g1, eye, lower=True)
    y1 = jnp.concatenate([col1, cT1], axis=0) - times_inv_t(
        jnp.concatenate([x0r, x0c], axis=0), x01)
    x1 = times_inv_t(y1, g1i)
    x1r, x1c = x1[:tiles], x1[tiles:]

    left = jnp.concatenate([x0r, x1r], axis=-1).reshape(tiles * width, 2 * width)
    right = jnp.concatenate([x0c, x1c], axis=-1).reshape(ucount * width, 2 * width)
    prod = jnp.dot(left, right.T, precision=HIGH, preferred_element_type=jnp.float32)
    upd = work - prod.reshape(tiles, width, ucount, width)
    irow = block_rows[:, None, None]
    p0r = jnp.where(irow > 0, x0r, jnp.where(irow == 0, g0[None], 0.0))
    p1r = jnp.where(irow > 1, x1r, jnp.where(irow == 1, g1[None], 0.0))
    jcol = block_cols[None, None, :, None]
    upd = jnp.where(block_rows[:, None, None, None] < 2, 0.0, upd)
    work = jnp.where(jcol == 0, p0r[:, :, None, :], jnp.where(jcol == 1, p1r[:, :, None, :], upd))
    return work.reshape(tiles, 1, width, ucount, 1, width)


def solution(mesh):
    in_specs = (P(None, "row", None, None, "col", None),)
    out_specs = P(None, "row", None, None, "col", None)
    return jax.shard_map(
        per_device, mesh=mesh, in_specs=in_specs, out_specs=out_specs, check_vma=False
    )
```

time: 425 us -> 383 us (0.901)
  local copies, waits for them, and re-layouts: 105 us -> 54.5 us
  starting transfers between devices: 69 us -> 81.5 us
  waiting for transfers between devices: 69.3 us -> 64 us
  matrix products: 29.9 us -> 34.3 us
    unnamed x138 -> x84, local copies, waits for them, and re-layouts: 51.2 us -> 10.8 us
    ppermute x0 -> x7, starting transfers between devices: none -> 21 us  [per_device(): lax.ppermute(blk, 'row', [(0, s), (1, (1 + s) % nrow)])]
    all_gather x1, waiting for transfers between devices: 15.1 us -> 0.02 us  [per_device(): cg = lax.all_gather(cmine, 'row')]
    dot_general x3 -> x4, matrix products: 16.6 us -> 28.4 us  [the longest x3 15.5 us: times_inv_t(): jnp.einsum('nab,cb->nac', y, ginv, precision=HIGH, preferred_element_type...]
    all_gather x1, waiting for transfers between devices: 49 us -> 58.2 us  [per_device(): rg = lax.all_gather(jnp.concatenate([rmine, lmine], axis=0), 'col')]
    ppermute x33, starting transfers between devices: 68.9 us -> 60.5 us  [prescatter(): got = got + lax.ppermute(pieces[q], axis, moved)]
    another operation x6, matrix products: 10.2 us -> 1.75 us  [the longest x3 0.88 us: per_device(): g1i = jax.scipy.linalg.solve_triangular(g1, eye, lower=True)]
    select_n x6 -> x2, local copies, waits for them, and re-layouts: 14 us -> 6.17 us  [the longest x1 3.13 us: per_device(): p1r = jnp.where(irow > 1, x1r, jnp.where(irow == 1, g1[None], 0.0))]
  transfers between devices with their start and end apart: 35 -> 42, of which waited for: 4 -> 3; matrix products, arithmetic and copies ran while one was open for 4% -> 5% of each run, Pallas kernels for 0% -> 0%
where the time goes in v2:
time: 383 us; the launch traced here: 377 us
  other arithmetic  126 us (33%)
  starting transfers between devices  81.5 us (21%)
  waiting for transfers between devices  64 us (17%)
  local copies, waits for them, and re-layouts  54.5 us (14%)
  matrix products  34.3 us (9%)
  between operations  17.4 us (5%)
    ppermute x33, starting transfers between devices, prescatter(): got = got + lax.ppermute(pieces[q], axis, moved)  60.5 us
    all_gather x1, waiting for transfers between devices, per_device(): rg = lax.all_gather(jnp.concatenate([rmine, lmine], axis=0), 'col')  58.2 us
    another operation x7, other arithmetic, per_device(): g1 = jnp.linalg.cholesky(a11u)  34.7 us
    another operation x6, other arithmetic, per_device(): g0 = jnp.linalg.cholesky(a00)  34 us
    another operation x2, other arithmetic, per_device(): g1i = jax.scipy.linalg.solve_triangular(g1, eye, lower=True)  22.4 us
    ppermute x7, starting transfers between devices, per_device(): lax.ppermute(blk, 'row', [(0, s), (1, (1 + s) % nrow)])  21 us
    another operation x3, other arithmetic, per_device(): g0i = jax.scipy.linalg.solve_triangular(g0, eye, lower=True)  20.6 us
    dot_general x3, matrix products, times_inv_t(): jnp.einsum('nab,cb->nac', y, ginv, precision=HIGH, preferred_element_type...  15.5 us
  transfers between devices with their start and end apart: 42, of which 3 were waited for; matrix products, arithmetic and copies ran while one was open for 5% of the time, Pallas kernels for 0%

profile of v2, /device:TPU:1, one launch (start us, length us, event | category | flops | bytes accessed | tf_op | source)
XLA Modules:
  0.0 377.3 jit_solution(4239050328824280230)
XLA Ops:
  6.5 2.7 copy.40
  9.3 2.0 copy-done.1
  12.0 8.3 %collective-permute-start.21 = (f32[256,256]{1,0:T(8,128)}, f32[256,256]{1,0:T(8,128)S(1)}, u32[]{:S(2)}, u32[]{:S(2)}) collective-permute-start(f32[256,256]{1,0:T(8,128)} %slice_bitcast_fusion.2), channel_id=1, source_target_pairs={{0,224},{32,0},{1,225},{33,1},{2,226},{34,2},{3,227},{35,3},{4,228... | collective-permute-start | bytes 786440 | tf_op jit(solution)/shard_map/ppermute | solution.py:46
  20.3 2.0 collective-permute-start.15
  23.5 1.9 collective-permute-start.37
  25.5 1.9 collective-permute-start.39
  27.4 1.9 collective-permute-start.38
  29.3 1.8 slice.300
  33.7 4.6 %collective-permute-start.19 = (f32[256,256]{1,0:T(8,128)}, f32[256,256]{1,0:T(8,128)S(1)}, u32[]{:S(2)}, u32[]{:S(2)}) collective-permute-start(f32[256,256]{1,0:T(8,128)} %slice_bitcast_fusion.2), channel_id=1, source_target_pairs={{0,160},{32,192},{1,161},{33,193},{2,162},{34,194},{3,163},{35,195... | collective-permute-start | bytes 786440 | tf_op jit(solution)/shard_map/ppermute | solution.py:46
  38.4 2.0 collective-permute-start.16
  47.0 3.1 collective-permute-done.17
  50.1 3.1 collective-permute-start
  53.2 2.5 collective-permute-done.18
  55.7 6.8 %collective-permute-start.14 = (f32[128,256]{1,0:T(8,128)}, f32[128,256]{1,0:T(8,128)S(1)}, u32[]{:S(2)}, u32[]{:S(2)}) collective-permute-start(f32[128,256]{1,0:T(8,128)} %get-tuple-element.59), channel_id=1, source_target_pairs={{0,30},{1,31},{32,62},{33,63},{64,94},{65,95},{96,126},{97,127},{1... | collective-permute-start | bytes 393224 | tf_op jit(solution)/shard_map/ppermute | solution.py:16
  62.6 4.3 %collective-permute-start.13 = (f32[128,256]{1,0:T(8,128)S(1)}, f32[128,256]{1,0:T(8,128)S(1)}, u32[]{:S(2)}, u32[]{:S(2)}) collective-permute-start(f32[128,256]{1,0:T(8,128)S(1)} %copy-done.24), channel_id=1, source_target_pairs={{0,28},{1,29},{32,60},{33,61},{64,92},{65,93},{96,124},{97,125},{1... | collective-permute-start | bytes 393224 | tf_op jit(solution)/shard_map/ppermute | solution.py:16
  87.2 1.9 collective-permute-start.35
  89.1 1.9 collective-permute-start.34
  91.0 1.9 collective-permute-start.33
  93.6 1.9 collective-permute-start.32
  96.2 1.9 collective-permute-start.31
  98.1 1.9 collective-permute-start.30
  99.9 1.9 collective-permute-start.22
  101.9 1.9 collective-permute-start.28
  109.1 1.8 collective-permute-start.23
  118.8 58.2 %all-gather.5.cloned.1.call-done = f32[5120,256]{1,0:T(8,128)} async-done(((f32[160,256]{1,0:T(8,128)}), f32[5120,256]{1,0:T(8,128)}) %all-gather.5.cloned.1.call-update) | async-done | bytes 5242896 | tf_op jit(solution)/shard_map/all_gather | solution.py:59
  177.0 2.0 fusion.57
  179.0 4.7 %fusion.58 = (f32[16,1,128,256]{3,2,1,0:T(8,128)}, f32[16,1,128,256]{3,2,1,0:T(8,128)}) fusion(f32[16,2,160,256]{3,2,1,0:T(8,128)} %bitcast.161), kind=kLoop, calls=%fused_computation.129 | loop fusion | bytes 8388608 | tf_op jit(solution)/shard_map/slice | solution.py:63
  183.9 11.7 %cholesky.130 = f32[128,128]{1,0:T(8,128)S(1)} custom-call(f32[128,128]{1,0:T(8,128)S(1)} %cholesky.194), custom_call_target="Cholesky" | custom-call | tf_op jit(solution)/shard_map/jit(cholesky)/cholesky | solution.py:80
  195.6 9.8 %custom-call.13 = f32[1,128,128]{1,2,0:T(8,128)S(1)} custom-call(f32[1,128,128]{2,1,0:T(8,128)S(1)} %get-tuple-element.104), custom_call_target="InvertDiagBlocksLowerTriangular" | custom-call | tf_op jit(solution)/shard_map/jit(cholesky)/cholesky | solution.py:80
  205.9 11.7 %cholesky.147 = f32[128,128]{1,0:T(8,128)S(1)} custom-call(f32[128,128]{1,0:T(8,128)S(1)} %convolution_subtract_fusion.4), custom_call_target="Cholesky" | custom-call | tf_op jit(solution)/shard_map/jit(cholesky)/cholesky | solution.py:80
  220.4 4.0 %while.4 = (s32[]{:T(128)}, f32[256,256]{1,0:T(8,128)S(1)}, s32[2,2]{1,0:T(2,128)S(1)}, f32[2,128,128]{2,1,0:T(8,128)S(1)}, s32[]{:T(128)}) while((s32[]{:T(128)}, f32[256,256]{1,0:T(8,128)S(1)}, s32[2,2]{1,0:T(2,128)S(1)}, f32[2,128,128]{2,1,0:T(8,128)S(1)}, s32[]{:T(128)}) %tuple.88), condition=%wide.while_cond, body=%wide.while_body.sunk | while | flops 2 | bytes 131189 | solution.py:81
  224.4 19.8 %custom-call.14 = f32[2,128,128]{1,2,0:T(8,128)S(1)} custom-call(f32[2,128,128]{2,1,0:T(8,128)S(1)} %get-tuple-element.21), custom_call_target="InvertDiagBlocksLowerTriangular" | custom-call | tf_op jit(solution)/shard_map/jit(_solve_triangular)/triangular_solve | solution.py:81
  245.2 4.5 %fusion.3 = f32[11,256,256]{1,2,0:T(8,128)S(1)} fusion(f32[1,256,256]{2,1,0:T(8,128)} %bitcast.165, f32[1,256,256]{2,1,0:T(8,128)} %get-tuple-element.116, f32[1,256,256]{2,1,0:T(8,128)} %get-tuple-element.115, f32[8,256,256]{2,1,0:T(8,128)} %bitcast.158, f32[128,256]{1,0:T(8,128)S(1)} %fusion.44, f32[128,256]{1,0:T(8,128)S(1)} %fusion.37), kind=kOutput, calls=%fused_computation.10 | convolution fusion | flops 2216820736 | bytes 6029312 | tf_op jit(solution)/shard_map/nab,cb->nac/dot_general | solution.py:77
  249.7 5.7 %fusion.23 = f32[10,256,256]{2,1,0:T(8,128)} fusion(f32[11,256,256]{1,2,0:T(8,128)S(1)} %fusion.3), kind=kOutput, calls=%fused_computation.47 | convolution fusion | flops 2013265920 | bytes 5767168 | tf_op jit(solution)/shard_map/nab,cb->nac/dot_general | solution.py:77
  256.3 1.8 copy.20
  262.2 11.9 %cholesky.164 = f32[128,128]{1,0:T(8,128)S(1)} custom-call(f32[128,128]{1,0:T(8,128)S(1)} %cholesky.197), custom_call_target="Cholesky" | custom-call | tf_op jit(solution)/shard_map/jit(cholesky)/cholesky | solution.py:85
  274.7 9.8 %custom-call.15 = f32[1,128,128]{1,2,0:T(8,128)S(1)} custom-call(f32[1,128,128]{2,1,0:T(8,128)S(1)} %get-tuple-element.100), custom_call_target="InvertDiagBlocksLowerTriangular" | custom-call | tf_op jit(solution)/shard_map/jit(cholesky)/cholesky | solution.py:85
  286.7 11.7 %cholesky.181 = f32[128,128]{1,0:T(8,128)S(1)} custom-call(f32[128,128]{1,0:T(8,128)S(1)} %convolution_subtract_fusion.3), custom_call_target="Cholesky" | custom-call | tf_op jit(solution)/shard_map/jit(cholesky)/cholesky | solution.py:85
  301.9 1.8 copy.25
  303.7 4.9 %while.5 = (s32[]{:T(128)}, f32[256,256]{1,0:T(8,128)S(1)}, s32[2,2]{1,0:T(2,128)}, f32[2,128,128]{2,1,0:T(8,128)S(1)}, s32[]{:T(128)}) while((s32[]{:T(128)}, f32[256,256]{1,0:T(8,128)S(1)}, s32[2,2]{1,0:T(2,128)}, f32[2,128,128]{2,1,0:T(8,128)S(1)}, s32[]{:T(128)}) %tuple.98), condition=%wide.while_cond.clone, body=%wide.while_body.clone.sunk | while | flops 2 | bytes 131189 | solution.py:86
  309.3 20.7 %custom-call.16 = f32[2,128,128]{1,2,0:T(8,128)S(1)} custom-call(f32[2,128,128]{2,1,0:T(8,128)} %copy-done.29), custom_call_target="InvertDiagBlocksLowerTriangular" | custom-call | tf_op jit(solution)/shard_map/jit(_solve_triangular)/triangular_solve | solution.py:86
  331.0 5.3 %fusion.11 = f32[10,256,256]{1,2,0:T(8,128)S(1)} fusion(f32[10,256,256]{2,1,0:T(8,128)} %fusion.23, f32[1,256,256]{2,1,0:T(8,128)} %get-tuple-element.74, f32[1,256,256]{2,1,0:T(8,128)} %get-tuple-element.73, f32[8,256,256]{2,1,0:T(8,128)} %bitcast.159, f32[128,256]{1,0:T(8,128)S(1)} %fusion.40, f32[128,256]{1,0:T(8,128)S(1)} %fusion.35), kind=kOutput, calls=%fused_computation.19 | convolution fusion | flops 2015297536 | bytes 8126464 | tf_op jit(solution)/shard_map/nab,cb->nac/dot_general | solution.py:77
  337.7 2.3 select_select_fusion.1
  340.1 3.0 copy.21
  343.1 2.3 select_select_fusion
  345.4 3.1 copy.26
  348.6 12.9 %select_bitcast_fusion = f32[8,1,256,2,1,256]{5,2,3,0,4,1:T(8,128)} fusion(f32[8,256,256]{1,2,0:T(8,128)} %get-tuple-element.57, f32[8,256,256]{1,2,0:T(8,128)S(1)} %copy-done.4, f32[8,256,256]{2,1,0:T(8,128)} %copy.26, f32[8,256,256]{2,1,0:T(8,128)} %copy.21, pred[8]{0:T(512)(128)(4,1)S(1)} %get-tuple-element.109, pred[2]{0:T(512)(128)(4,1)S(1)} %get-tuple-element.113, ...), kind=kOutput, calls=%fused_computation.9 | convolution fusion | flops 6447955968 | bytes 17825804 | tf_op jit(solution)/shard_map/dot_general | solution.py:94
  361.5 8.5 %copy.29 = f32[8,1,256,2,1,256]{5,4,3,2,1,0:T(1,128)} copy(f32[8,1,256,2,1,256]{5,2,3,0,4,1:T(8,128)} %select_bitcast_fusion) | data formatting | bytes 8388608 | tf_op jit(solution)/shard_map/reshape | solution.py:102
  (216 shorter events, 70.3 us)
Async XLA Ops:
  6.5 109.2 %all-gather.7.cloned.1.call-start = ((), (), s32[]{:S(2)}) async-start(), calls=%async_computation.1 | async-start | bytes 1179648 | tf_op jit(solution)/shard_map/all_gather | solution.py:37
  12.0 56.2 %collective-permute-start.21 = (f32[256,256]{1,0:T(8,128)}, f32[256,256]{1,0:T(8,128)S(1)}, u32[]{:S(2)}, u32[]{:S(2)}) collective-permute-start(f32[256,256]{1,0:T(8,128)} %slice_bitcast_fusion.2), channel_id=1, source_target_pairs={{0,224},{32,0},{1,225},{33,1},{2,226},{34,2},{3,227},{35,3},{4,228... | collective-permute-start | bytes 786440 | tf_op jit(solution)/shard_map/ppermute | solution.py:46
  20.3 21.9 %collective-permute-start.15 = (f32[256,256]{1,0:T(8,128)}, f32[256,256]{1,0:T(8,128)}, u32[]{:S(2)}, u32[]{:S(2)}) collective-permute-start(f32[256,256]{1,0:T(8,128)} %slice_bitcast_fusion.2), channel_id=1, source_target_pairs={{0,32},{32,64},{1,33},{33,65},{2,34},{34,66},{3,35},{35,67},{4,36}... | collective-permute-start | bytes 786440 | tf_op jit(solution)/shard_map/ppermute | solution.py:46
  23.5 8.9 %collective-permute-start.37 = (f32[128,256]{0,1:T(8,128)S(1)}, f32[128,256]{0,1:T(8,128)}, u32[]{:S(2)}, u32[]{:S(2)}) collective-permute-start(f32[128,256]{0,1:T(8,128)S(1)} %get-tuple-element.79), channel_id=1, source_target_pairs={{0,224},{32,64},{1,225},{33,65},{2,226},{34,66},{3,227},{35,67},{4... | collective-permute-start | bytes 393224 | tf_op jit(solution)/shard_map/ppermute | solution.py:16
  25.5 8.2 %collective-permute-start.39 = (f32[128,256]{0,1:T(8,128)S(1)}, f32[128,256]{0,1:T(8,128)}, u32[]{:S(2)}, u32[]{:S(2)}) collective-permute-start(f32[128,256]{0,1:T(8,128)S(1)} %get-tuple-element.80), channel_id=1, source_target_pairs={{0,160},{32,128},{1,161},{33,129},{2,162},{34,130},{3,163},{35,131... | collective-permute-start | bytes 393224 | tf_op jit(solution)/shard_map/ppermute | solution.py:16
  27.4 10.9 %collective-permute-start.38 = (f32[128,256]{0,1:T(8,128)}, f32[128,256]{0,1:T(8,128)}, u32[]{:S(2)}, u32[]{:S(2)}) collective-permute-start(f32[128,256]{0,1:T(8,128)} %get-tuple-element.81), channel_id=1, source_target_pairs={{0,192},{32,96},{1,193},{33,97},{2,194},{34,98},{3,195},{35,99},{4... | collective-permute-start | bytes 393224 | tf_op jit(solution)/shard_map/ppermute | solution.py:16
  32.4 34.5 %collective-permute-start.20 = (f32[256,256]{1,0:T(8,128)}, f32[256,256]{1,0:T(8,128)S(1)}, u32[]{:S(2)}, u32[]{:S(2)}) collective-permute-start(f32[256,256]{1,0:T(8,128)} %slice_bitcast_fusion.2), channel_id=1, source_target_pairs={{0,192},{32,224},{1,193},{33,225},{2,194},{34,226},{3,195},{35,227... | collective-permute-start | bytes 786440 | tf_op jit(solution)/shard_map/ppermute | solution.py:46
  33.7 28.8 %collective-permute-start.19 = (f32[256,256]{1,0:T(8,128)}, f32[256,256]{1,0:T(8,128)S(1)}, u32[]{:S(2)}, u32[]{:S(2)}) collective-permute-start(f32[256,256]{1,0:T(8,128)} %slice_bitcast_fusion.2), channel_id=1, source_target_pairs={{0,160},{32,192},{1,161},{33,193},{2,162},{34,194},{3,163},{35,195... | collective-permute-start | bytes 786440 | tf_op jit(solution)/shard_map/ppermute | solution.py:46
  38.4 6.3 %collective-permute-start.16 = (f32[256,256]{1,0:T(8,128)}, f32[256,256]{1,0:T(8,128)}, u32[]{:S(2)}, u32[]{:S(2)}) collective-permute-start(f32[256,256]{1,0:T(8,128)} %slice_bitcast_fusion.2), channel_id=1, source_target_pairs={{0,64},{32,96},{1,65},{33,97},{2,66},{34,98},{3,67},{35,99},{4,68}... | collective-permute-start | bytes 786440 | tf_op jit(solution)/shard_map/ppermute | solution.py:46
  42.1 134.9 %all-gather.5.cloned.1.call-start = ((), (), s32[]{:S(2)}) async-start(), calls=%async_computation | async-start | bytes 5406720 | tf_op jit(solution)/shard_map/all_gather | solution.py:59
  42.2 7.9 %collective-permute-start.17 = (f32[256,256]{1,0:T(8,128)}, f32[256,256]{1,0:T(8,128)S(1)}, u32[]{:S(2)}, u32[]{:S(2)}) collective-permute-start(f32[256,256]{1,0:T(8,128)} %slice_bitcast_fusion.2), channel_id=1, source_target_pairs={{0,96},{32,128},{1,97},{33,129},{2,98},{34,130},{3,99},{35,131},{4... | collective-permute-start | bytes 786440 | tf_op jit(solution)/shard_map/ppermute | solution.py:46
  44.6 11.0 %collective-permute-start.18 = (f32[256,256]{1,0:T(8,128)}, f32[256,256]{1,0:T(8,128)S(1)}, u32[]{:S(2)}, u32[]{:S(2)}) collective-permute-start(f32[256,256]{1,0:T(8,128)} %slice_bitcast_fusion.2), channel_id=1, source_target_pairs={{0,128},{32,160},{1,129},{33,161},{2,130},{34,162},{3,131},{35,163... | collective-permute-start | bytes 786440 | tf_op jit(solution)/shard_map/ppermute | solution.py:46
  46.9 31.7 %copy-start.15 = (f32[128,256]{1,0:T(8,128)S(1)}, f32[128,256]{1,0:T(8,128)}, u32[]{:S(2)}) copy-start(f32[128,256]{1,0:T(8,128)} %get-tuple-element.69) | copy-start | bytes 393220
  46.9 33.0 %copy-start.14 = (f32[128,256]{1,0:T(8,128)S(1)}, f32[128,256]{1,0:T(8,128)}, u32[]{:S(2)}) copy-start(f32[128,256]{1,0:T(8,128)} %get-tuple-element.70) | copy-start | bytes 393220
  46.9 34.4 %copy-start.13 = (f32[128,256]{1,0:T(8,128)S(1)}, f32[128,256]{1,0:T(8,128)}, u32[]{:S(2)}) copy-start(f32[128,256]{1,0:T(8,128)} %get-tuple-element.71) | copy-start | bytes 393220
  50.1 19.6 %collective-permute-start = (f32[128,256]{1,0:T(8,128)}, f32[128,256]{1,0:T(8,128)S(1)}, u32[]{:S(2)}, u32[]{:S(2)}) collective-permute-start(f32[128,256]{1,0:T(8,128)} %get-tuple-element.58), channel_id=1, source_target_pairs={{0,2},{1,3},{32,34},{33,35},{64,66},{65,67},{96,98},{97,99},{128,1... | collective-permute-start | bytes 393224 | tf_op jit(solution)/shard_map/ppermute | solution.py:16
  55.7 15.3 %collective-permute-start.14 = (f32[128,256]{1,0:T(8,128)}, f32[128,256]{1,0:T(8,128)S(1)}, u32[]{:S(2)}, u32[]{:S(2)}) collective-permute-start(f32[128,256]{1,0:T(8,128)} %get-tuple-element.59), channel_id=1, source_target_pairs={{0,30},{1,31},{32,62},{33,63},{64,94},{65,95},{96,126},{97,127},{1... | collective-permute-start | bytes 393224 | tf_op jit(solution)/shard_map/ppermute | solution.py:16
  62.6 9.7 %collective-permute-start.13 = (f32[128,256]{1,0:T(8,128)S(1)}, f32[128,256]{1,0:T(8,128)S(1)}, u32[]{:S(2)}, u32[]{:S(2)}) collective-permute-start(f32[128,256]{1,0:T(8,128)S(1)} %copy-done.24), channel_id=1, source_target_pairs={{0,28},{1,29},{32,60},{33,61},{64,92},{65,93},{96,124},{97,125},{1... | collective-permute-start | bytes 393224 | tf_op jit(solution)/shard_map/ppermute | solution.py:16
  66.9 6.7 %collective-permute-start.12 = (f32[128,256]{1,0:T(8,128)S(1)}, f32[128,256]{1,0:T(8,128)S(1)}, u32[]{:S(2)}, u32[]{:S(2)}) collective-permute-start(f32[128,256]{1,0:T(8,128)S(1)} %copy-done.22), channel_id=1, source_target_pairs={{0,26},{1,27},{32,58},{33,59},{64,90},{65,91},{96,122},{97,123},{1... | collective-permute-start | bytes 393224 | tf_op jit(solution)/shard_map/ppermute | solution.py:16
  68.3 6.6 %collective-permute-start.11 = (f32[128,256]{1,0:T(8,128)S(1)}, f32[128,256]{1,0:T(8,128)S(1)}, u32[]{:S(2)}, u32[]{:S(2)}) collective-permute-start(f32[128,256]{1,0:T(8,128)S(1)} %copy-done.21), channel_id=1, source_target_pairs={{0,24},{1,25},{32,56},{33,57},{64,88},{65,89},{96,120},{97,121},{1... | collective-permute-start | bytes 393224 | tf_op jit(solution)/shard_map/ppermute | solution.py:16
  69.6 7.7 %collective-permute-start.10 = (f32[128,256]{1,0:T(8,128)}, f32[128,256]{1,0:T(8,128)S(1)}, u32[]{:S(2)}, u32[]{:S(2)}) collective-permute-start(f32[128,256]{1,0:T(8,128)} %get-tuple-element.63), channel_id=1, source_target_pairs={{0,22},{1,23},{32,54},{33,55},{64,86},{65,87},{96,118},{97,119},{1... | collective-permute-start | bytes 393224 | tf_op jit(solution)/shard_map/ppermute | solution.py:16
  71.0 7.7 %collective-permute-start.9 = (f32[128,256]{1,0:T(8,128)}, f32[128,256]{1,0:T(8,128)S(1)}, u32[]{:S(2)}, u32[]{:S(2)}) collective-permute-start(f32[128,256]{1,0:T(8,128)} %get-tuple-element.64), channel_id=1, source_target_pairs={{0,20},{1,21},{32,52},{33,53},{64,84},{65,85},{96,116},{97,117},{1... | collective-permute-start | bytes 393224 | tf_op jit(solution)/shard_map/ppermute | solution.py:16
  72.3 7.7 %collective-permute-start.8 = (f32[128,256]{1,0:T(8,128)}, f32[128,256]{1,0:T(8,128)S(1)}, u32[]{:S(2)}, u32[]{:S(2)}) collective-permute-start(f32[128,256]{1,0:T(8,128)} %get-tuple-element.65), channel_id=1, source_target_pairs={{0,18},{1,19},{32,50},{33,51},{64,82},{65,83},{96,114},{97,115},{1... | collective-permute-start | bytes 393224 | tf_op jit(solution)/shard_map/ppermute | solution.py:16
  73.6 7.7 %collective-permute-start.7 = (f32[128,256]{1,0:T(8,128)}, f32[128,256]{1,0:T(8,128)S(1)}, u32[]{:S(2)}, u32[]{:S(2)}) collective-permute-start(f32[128,256]{1,0:T(8,128)} %get-tuple-element.66), channel_id=1, source_target_pairs={{0,16},{1,17},{32,48},{33,49},{64,80},{65,81},{96,112},{97,113},{1... | collective-permute-start | bytes 393224 | tf_op jit(solution)/shard_map/ppermute | solution.py:16
  74.9 7.7 %collective-permute-start.6 = (f32[128,256]{1,0:T(8,128)}, f32[128,256]{1,0:T(8,128)S(1)}, u32[]{:S(2)}, u32[]{:S(2)}) collective-permute-start(f32[128,256]{1,0:T(8,128)} %get-tuple-element.67), channel_id=1, source_target_pairs={{0,14},{1,15},{32,46},{33,47},{64,78},{65,79},{96,110},{97,111},{1... | collective-permute-start | bytes 393224 | tf_op jit(solution)/shard_map/ppermute | solution.py:16
  76.2 34.7 %copy-start.12 = (f32[128,256]{1,0:T(8,128)S(1)}, f32[128,256]{1,0:T(8,128)}, u32[]{:S(2)}) copy-start(f32[128,256]{1,0:T(8,128)} %copy-done.11) | copy-start | bytes 393220
  76.2 34.7 %copy-start.17 = (f32[128,256]{1,0:T(8,128)S(1)}, f32[128,256]{1,0:T(8,128)}, u32[]{:S(2)}) copy-start(f32[128,256]{1,0:T(8,128)} %copy-done.16) | copy-start | bytes 393220
  77.3 7.3 %collective-permute-start.5 = (f32[128,256]{1,0:T(8,128)S(1)}, f32[128,256]{1,0:T(8,128)S(1)}, u32[]{:S(2)}, u32[]{:S(2)}) collective-permute-start(f32[128,256]{1,0:T(8,128)S(1)} %copy-done.18), channel_id=1, source_target_pairs={{0,12},{1,13},{32,44},{33,45},{64,76},{65,77},{96,108},{97,109},{1... | collective-permute-start | bytes 393224 | tf_op jit(solution)/shard_map/ppermute | solution.py:16
  78.7 7.2 %collective-permute-start.4 = (f32[128,256]{1,0:T(8,128)S(1)}, f32[128,256]{1,0:T(8,128)S(1)}, u32[]{:S(2)}, u32[]{:S(2)}) collective-permute-start(f32[128,256]{1,0:T(8,128)S(1)} %copy-done.15), channel_id=1, source_target_pairs={{0,10},{1,11},{32,42},{33,43},{64,74},{65,75},{96,106},{97,107},{1... | collective-permute-start | bytes 393224 | tf_op jit(solution)/shard_map/ppermute | solution.py:16
  80.0 7.2 %collective-permute-start.3 = (f32[128,256]{1,0:T(8,128)S(1)}, f32[128,256]{1,0:T(8,128)S(1)}, u32[]{:S(2)}, u32[]{:S(2)}) collective-permute-start(f32[128,256]{1,0:T(8,128)S(1)} %copy-done.14), channel_id=1, source_target_pairs={{0,8},{1,9},{32,40},{33,41},{64,72},{65,73},{96,104},{97,105},{128... | collective-permute-start | bytes 393224 | tf_op jit(solution)/shard_map/ppermute | solution.py:16
  81.3 7.8 %collective-permute-start.2 = (f32[128,256]{1,0:T(8,128)S(1)}, f32[128,256]{1,0:T(8,128)S(1)}, u32[]{:S(2)}, u32[]{:S(2)}) collective-permute-start(f32[128,256]{1,0:T(8,128)S(1)} %copy-done.13), channel_id=1, source_target_pairs={{0,6},{1,7},{32,38},{33,39},{64,70},{65,71},{96,102},{97,103},{128... | collective-permute-start | bytes 393224 | tf_op jit(solution)/shard_map/ppermute | solution.py:16
  82.7 8.4 %collective-permute-start.1 = (f32[128,256]{1,0:T(8,128)S(1)}, f32[128,256]{1,0:T(8,128)S(1)}, u32[]{:S(2)}, u32[]{:S(2)}) collective-permute-start(f32[128,256]{1,0:T(8,128)S(1)} %get-tuple-element.72), channel_id=1, source_target_pairs={{0,4},{1,5},{32,36},{33,37},{64,68},{65,69},{96,100},{97,101},{128... | collective-permute-start | bytes 393224 | tf_op jit(solution)/shard_map/ppermute | solution.py:16
  84.6 9.0 %collective-permute-start.29 = (f32[32,256]{1,0:T(8,128)S(1)}, f32[32,256]{1,0:T(8,128)S(1)}, u32[]{:S(2)}, u32[]{:S(2)}) collective-permute-start(f32[32,256]{1,0:T(8,128)S(1)} %get-tuple-element.89), channel_id=1, source_target_pairs={{0,16},{1,17},{32,48},{33,49},{64,80},{65,81},{96,112},{97,113},{1... | collective-permute-start | bytes 98312 | tf_op jit(solution)/shard_map/ppermute | solution.py:16
  85.9 9.6 %collective-permute-start.36 = (f32[32,256]{1,0:T(8,128)S(1)}, f32[32,256]{1,0:T(8,128)S(1)}, u32[]{:S(2)}, u32[]{:S(2)}) collective-permute-start(f32[32,256]{1,0:T(8,128)S(1)} %get-tuple-element.90), channel_id=1, source_target_pairs={{0,30},{1,31},{32,62},{33,63},{64,94},{65,95},{96,126},{97,127},{1... | collective-permute-start | bytes 98312 | tf_op jit(solution)/shard_map/ppermute | solution.py:16
  87.2 10.8 %collective-permute-start.35 = (f32[32,256]{1,0:T(8,128)S(1)}, f32[32,256]{1,0:T(8,128)}, u32[]{:S(2)}, u32[]{:S(2)}) collective-permute-start(f32[32,256]{1,0:T(8,128)S(1)} %get-tuple-element.91), channel_id=1, source_target_pairs={{0,28},{1,29},{32,60},{33,61},{64,92},{65,93},{96,124},{97,125},{1... | collective-permute-start | bytes 98312 | tf_op jit(solution)/shard_map/ppermute | solution.py:16
  89.1 10.8 %collective-permute-start.34 = (f32[32,256]{1,0:T(8,128)S(1)}, f32[32,256]{1,0:T(8,128)}, u32[]{:S(2)}, u32[]{:S(2)}) collective-permute-start(f32[32,256]{1,0:T(8,128)S(1)} %get-tuple-element.92), channel_id=1, source_target_pairs={{0,26},{1,27},{32,58},{33,59},{64,90},{65,91},{96,122},{97,123},{1... | collective-permute-start | bytes 98312 | tf_op jit(solution)/shard_map/ppermute | solution.py:16
  91.0 10.8 %collective-permute-start.33 = (f32[32,256]{1,0:T(8,128)S(1)}, f32[32,256]{1,0:T(8,128)}, u32[]{:S(2)}, u32[]{:S(2)}) collective-permute-start(f32[32,256]{1,0:T(8,128)S(1)} %get-tuple-element.93), channel_id=1, source_target_pairs={{0,24},{1,25},{32,56},{33,57},{64,88},{65,89},{96,120},{97,121},{1... | collective-permute-start | bytes 98312 | tf_op jit(solution)/shard_map/ppermute | solution.py:16
  93.6 10.1 %collective-permute-start.32 = (f32[32,256]{1,0:T(8,128)}, f32[32,256]{1,0:T(8,128)}, u32[]{:S(2)}, u32[]{:S(2)}) collective-permute-start(f32[32,256]{1,0:T(8,128)} %get-tuple-element.94), channel_id=1, source_target_pairs={{0,22},{1,23},{32,54},{33,55},{64,86},{65,87},{96,118},{97,119},{1... | collective-permute-start | bytes 98312 | tf_op jit(solution)/shard_map/ppermute | solution.py:16
  96.2 9.0 %collective-permute-start.31 = (f32[32,256]{1,0:T(8,128)}, f32[32,256]{1,0:T(8,128)}, u32[]{:S(2)}, u32[]{:S(2)}) collective-permute-start(f32[32,256]{1,0:T(8,128)} %get-tuple-element.95), channel_id=1, source_target_pairs={{0,20},{1,21},{32,52},{33,53},{64,84},{65,85},{96,116},{97,117},{1... | collective-permute-start | bytes 98312 | tf_op jit(solution)/shard_map/ppermute | solution.py:16
  98.1 8.4 %collective-permute-start.30 = (f32[32,256]{1,0:T(8,128)}, f32[32,256]{1,0:T(8,128)}, u32[]{:S(2)}, u32[]{:S(2)}) collective-permute-start(f32[32,256]{1,0:T(8,128)} %get-tuple-element.96), channel_id=1, source_target_pairs={{0,18},{1,19},{32,50},{33,51},{64,82},{65,83},{96,114},{97,115},{1... | collective-permute-start | bytes 98312 | tf_op jit(solution)/shard_map/ppermute | solution.py:16
  99.9 7.8 %collective-permute-start.22 = (f32[32,256]{1,0:T(8,128)}, f32[32,256]{1,0:T(8,128)}, u32[]{:S(2)}, u32[]{:S(2)}) collective-permute-start(f32[32,256]{1,0:T(8,128)} %get-tuple-element.82), channel_id=1, source_target_pairs={{0,2},{1,3},{32,34},{33,35},{64,66},{65,67},{96,98},{97,99},{128,1... | collective-permute-start | bytes 98312 | tf_op jit(solution)/shard_map/ppermute | solution.py:16
  101.9 7.3 %collective-permute-start.28 = (f32[32,256]{1,0:T(8,128)}, f32[32,256]{1,0:T(8,128)}, u32[]{:S(2)}, u32[]{:S(2)}) collective-permute-start(f32[32,256]{1,0:T(8,128)} %get-tuple-element.83), channel_id=1, source_target_pairs={{0,14},{1,15},{32,46},{33,47},{64,78},{65,79},{96,110},{97,111},{1... | collective-permute-start | bytes 98312 | tf_op jit(solution)/shard_map/ppermute | solution.py:16
  103.8 8.6 %collective-permute-start.27 = (f32[32,256]{1,0:T(8,128)}, f32[32,256]{1,0:T(8,128)S(1)}, u32[]{:S(2)}, u32[]{:S(2)}) collective-permute-start(f32[32,256]{1,0:T(8,128)} %get-tuple-element.84), channel_id=1, source_target_pairs={{0,12},{1,13},{32,44},{33,45},{64,76},{65,77},{96,108},{97,109},{1... | collective-permute-start | bytes 98312 | tf_op jit(solution)/shard_map/ppermute | solution.py:16
  105.2 7.2 %collective-permute-start.26 = (f32[32,256]{1,0:T(8,128)S(1)}, f32[32,256]{1,0:T(8,128)S(1)}, u32[]{:S(2)}, u32[]{:S(2)}) collective-permute-start(f32[32,256]{1,0:T(8,128)S(1)} %get-tuple-element.85), channel_id=1, source_target_pairs={{0,10},{1,11},{32,42},{33,43},{64,74},{65,75},{96,106},{97,107},{1... | collective-permute-start | bytes 98312 | tf_op jit(solution)/shard_map/ppermute | solution.py:16
  106.5 5.9 %collective-permute-start.25 = (f32[32,256]{1,0:T(8,128)S(1)}, f32[32,256]{1,0:T(8,128)S(1)}, u32[]{:S(2)}, u32[]{:S(2)}) collective-permute-start(f32[32,256]{1,0:T(8,128)S(1)} %get-tuple-element.86), channel_id=1, source_target_pairs={{0,8},{1,9},{32,40},{33,41},{64,72},{65,73},{96,104},{97,105},{128... | collective-permute-start | bytes 98312 | tf_op jit(solution)/shard_map/ppermute | solution.py:16
  107.8 4.6 %collective-permute-start.24 = (f32[32,256]{1,0:T(8,128)S(1)}, f32[32,256]{1,0:T(8,128)S(1)}, u32[]{:S(2)}, u32[]{:S(2)}) collective-permute-start(f32[32,256]{1,0:T(8,128)S(1)} %get-tuple-element.87), channel_id=1, source_target_pairs={{0,6},{1,7},{32,38},{33,39},{64,70},{65,71},{96,102},{97,103},{128... | collective-permute-start | bytes 98312 | tf_op jit(solution)/shard_map/ppermute | solution.py:16
  109.1 3.3 collective-permute-start.23
  249.7 88.0 %copy-start = (f32[11,256,256]{1,2,0:T(8,128)}, f32[11,256,256]{1,2,0:T(8,128)S(1)}, u32[]{:S(2)}) copy-start(f32[11,256,256]{1,2,0:T(8,128)S(1)} %fusion.3) | copy-start | bytes 8650756
  (35 other events, 270.6 us)
Sparse Core Ops, SparseCore 0:
  42.2 46.8 all-gather.6
  114.2 62.7 all-gather.4

commit v3 on v2

--- a/solution.py
+++ b/solution.py
@@ -48,7 +48,20 @@
     from1 = lax.dynamic_index_in_dim(recv, (my_row + nrow - 2) % nrow, keepdims=False)
     a0c = jnp.where(my_row == 0, blk, from0)
     a1c = jnp.where(my_row == 1, blk, from1)
-    lead = jnp.concatenate([a0c, a1c], axis=0)
+    eye = jnp.eye(width, dtype=jnp.float32)
+    swap = lax.ppermute(jnp.where(my_col == 0, a0c, a1c), "col", [(0, 1), (1, 0)])
+    a00 = jnp.where(my_col == 0, a0c, swap)
+    a11 = jnp.where(my_col == 0, swap, a1c)
+    a10 = jnp.where(my_col == 0, a1c, a0c.T)
+    g0 = jnp.linalg.cholesky(a00)
+    g0i = jax.scipy.linalg.solve_triangular(g0, eye, lower=True)
+    x01 = jnp.dot(a10, g0i.T, precision=HIGH, preferred_element_type=jnp.float32)
+    a11u = a11 - jnp.dot(x01, x01.T, precision=HIGH, preferred_element_type=jnp.float32)
+    g1 = jnp.linalg.cholesky(a11u)
+    g1i = jax.scipy.linalg.solve_triangular(g1, eye, lower=True)
+    res = jnp.concatenate([g0i, x01, g1i], axis=0)
+    hres = res.shape[0] // 2
+    lead = jnp.where(my_col == 0, res[:hres], res[hres:])
     pcol = work[:, :, 0, :].reshape(tiles * width, width)
     npieces = ncol // 2
     rrows = pcol.shape[0] // npieces
@@ -61,32 +74,25 @@
 
     col0 = rg[:, 0, :rrows].reshape(tiles, width, width)
     col1 = rg[:, 1, :rrows].reshape(tiles, width, width)
-    lead0 = rg[:, 0, rrows:].reshape(2 * width, width)
-    lead1 = rg[:, 1, rrows:].reshape(2 * width, width)
-    a00 = lead0[:width]
-    a10 = lead0[width:]
-    a11 = lead1[width:]
+    resg = jnp.concatenate([rg[:, 0, rrows:].reshape(hres, width),
+                            rg[:, 1, rrows:].reshape(hres, width)], axis=0)
+    g0i_all = resg[:width]
+    x01_all = resg[width:2 * width]
+    g1i_all = resg[2 * width:]
 
     block_rows = jnp.arange(tiles, dtype=jnp.int32) * nrow + my_row
     block_cols = jnp.arange(ucount, dtype=jnp.int32) * ncol + my_col
     cT0 = jnp.stack([crow[0][u].T for u in range(ucount)])
     cT1 = jnp.stack([crow[1][u].T for u in range(ucount)])
-    eye = jnp.eye(width, dtype=jnp.float32)
 
     def times_inv_t(y, ginv):
         return jnp.einsum("nab,cb->nac", y, ginv, precision=HIGH,
                           preferred_element_type=jnp.float32)
 
-    g0 = jnp.linalg.cholesky(a00)
-    g0i = jax.scipy.linalg.solve_triangular(g0, eye, lower=True)
-    x0 = times_inv_t(jnp.concatenate([col0, cT0, a10[None]], axis=0), g0i)
-    x0r, x0c, x01 = x0[:tiles], x0[tiles:tiles + ucount], x0[tiles + ucount]
-    a11u = a11 - jnp.dot(x01, x01.T, precision=HIGH, preferred_element_type=jnp.float32)
-    g1 = jnp.linalg.cholesky(a11u)
-    g1i = jax.scipy.linalg.solve_triangular(g1, eye, lower=True)
-    y1 = jnp.concatenate([col1, cT1], axis=0) - times_inv_t(
-        jnp.concatenate([x0r, x0c], axis=0), x01)
-    x1 = times_inv_t(y1, g1i)
+    x0 = times_inv_t(jnp.concatenate([col0, cT0], axis=0), g0i_all)
+    x0r, x0c = x0[:tiles], x0[tiles:]
+    y1 = jnp.concatenate([col1, cT1], axis=0) - times_inv_t(x0, x01_all)
+    x1 = times_inv_t(y1, g1i_all)
     x1r, x1c = x1[:tiles], x1[tiles:]
 
     left = jnp.concatenate([x0r, x1r], axis=-1).reshape(tiles * width, 2 * width)

time: 383 us -> 377 us (0.984)
  starting transfers between devices: 81.5 us -> 98 us
  waiting for transfers between devices: 64 us -> 53.2 us
  local copies, waits for them, and re-layouts: 54.5 us -> 47.5 us
    all_gather x1, waiting for transfers between devices: 58.2 us -> 45.1 us  [per_device(): rg = lax.all_gather(jnp.concatenate([rmine, lmine], axis=0), 'col')]
    ppermute x33, starting transfers between devices: 60.5 us -> 72.7 us  [prescatter(): got = got + lax.ppermute(pieces[q], axis, moved)]
    dot_general x3, matrix products: 15.5 us -> 9.6 us  [times_inv_t(): jnp.einsum('nab,cb->nac', y, ginv, precision=HIGH, preferred_element_type...]
    ppermute x0 -> x1, starting transfers between devices: none -> 4.21 us  [per_device(): lax.ppermute(jnp.where(my_col == 0, a0c, a1c), 'col', [(0, 1), (1, 0)])]
    unnamed x84 -> x74, local copies, waits for them, and re-layouts: 10.8 us -> 11 us
  transfers between devices with their start and end apart: 42 -> 43, of which waited for: 3 -> 4; matrix products, arithmetic and copies ran while one was open for 5% -> 40% of each run, Pallas kernels for 0% -> 0%
where the time goes in v3:
time: 377 us; the launch traced here: 372 us
  other arithmetic  124 us (33%)
  starting transfers between devices  98 us (26%)
  waiting for transfers between devices  53.2 us (14%)
  local copies, waits for them, and re-layouts  47.5 us (13%)
  matrix products  31.7 us (8%)
  between operations  17.6 us (5%)
    ppermute x33, starting transfers between devices, prescatter(): got = got + lax.ppermute(pieces[q], axis, moved)  72.7 us
    all_gather x1, waiting for transfers between devices, per_device(): rg = lax.all_gather(jnp.concatenate([rmine, lmine], axis=0), 'col')  45.1 us
    another operation x7, other arithmetic, per_device(): g1 = jnp.linalg.cholesky(a11u)  34.7 us
    another operation x6, other arithmetic, per_device(): g0 = jnp.linalg.cholesky(a00)  34 us
    ppermute x7, starting transfers between devices, per_device(): lax.ppermute(blk, 'row', [(0, s), (1, (1 + s) % nrow)])  21.1 us
    another operation x3, other arithmetic, per_device(): g0i = jax.scipy.linalg.solve_triangular(g0, eye, lower=True)  20.8 us
    another operation x2, other arithmetic, per_device(): g1i = jax.scipy.linalg.solve_triangular(g1, eye, lower=True)  20.6 us
    dot_general x1, matrix products, per_device(): jnp.dot(left, right.T, precision=HIGH, preferred_element_type=jnp.float32)  12.6 us
  transfers between devices with their start and end apart: 43, of which 4 were waited for; matrix products, arithmetic and copies ran while one was open for 40% of the time, Pallas kernels for 0%

profile of v3, /device:TPU:1, one launch (start us, length us, event | category | flops | bytes accessed | tf_op | source)
XLA Modules:
  0.0 371.9 jit_solution(606623267664327905)
XLA Ops:
  6.5 2.7 copy.66
  9.3 8.3 %collective-permute-start.21 = (f32[256,256]{1,0:T(8,128)S(1)}, f32[256,256]{1,0:T(8,128)}, u32[]{:S(2)}, u32[]{:S(2)}) collective-permute-start(f32[256,256]{1,0:T(8,128)S(1)} %slice_bitcast_fusion.6), channel_id=1, source_target_pairs={{0,224},{32,0},{1,225},{33,1},{2,226},{34,2},{3,227},{35,3},{4,228... | collective-permute-start | bytes 786440 | tf_op jit(solution)/shard_map/ppermute | solution.py:46
  17.6 3.1 collective-permute-start.20
  20.7 2.0 collective-permute-start.19
  22.6 2.0 collective-permute-start.16
  24.6 3.1 collective-permute-start.15
  31.6 3.0 collective-permute-done.15
  40.4 1.9 collective-permute-start.38
  42.4 3.7 collective-permute-done.18
  46.0 22.0 %collective-permute-start.40 = (f32[128,256]{0,1:T(8,128)}, f32[128,256]{0,1:T(8,128)}, u32[]{:S(2)}, u32[]{:S(2)}) collective-permute-start(f32[128,256]{0,1:T(8,128)} %get-tuple-element.79), channel_id=1, source_target_pairs={{0,160},{32,128},{1,161},{33,129},{2,162},{34,130},{3,163},{35,131... | collective-permute-start | bytes 393224 | tf_op jit(solution)/shard_map/ppermute | solution.py:16
  68.1 1.9 collective-permute-start.39
  71.0 3.8 %collective-permute-start = (f32[128,256]{1,0:T(8,128)}, f32[128,256]{1,0:T(8,128)}, u32[]{:S(2)}, u32[]{:S(2)}) collective-permute-start(f32[128,256]{1,0:T(8,128)} %get-tuple-element.57), channel_id=1, source_target_pairs={{0,2},{1,3},{32,34},{33,35},{64,66},{65,67},{96,98},{97,99},{128,1... | collective-permute-start | bytes 393224 | tf_op jit(solution)/shard_map/ppermute | solution.py:16
  78.3 1.8 broadcast_select_fusion.2
  80.1 4.2 %collective-permute-start.22 = (f32[256,256]{1,0:T(8,128)}, f32[256,256]{1,0:T(8,128)S(1)}, u32[]{:S(2)}, u32[]{:S(2)}) collective-permute-start(f32[256,256]{1,0:T(8,128)} %get-tuple-element.43), channel_id=1, source_target_pairs={{0,1},{1,0},{32,33},{33,32},{64,65},{65,64},{96,97},{97,96},{128,1... | collective-permute-start | bytes 786440 | tf_op jit(solution)/shard_map/ppermute | solution.py:52
  84.3 2.0 collective-permute-start.14
  86.3 1.9 collective-permute-start.13
  88.2 1.9 collective-permute-start.12
  90.2 1.8 fusion.32
  92.0 2.1 collective-permute-start.11
  95.2 11.7 %cholesky.130 = f32[128,128]{1,0:T(8,128)S(1)} custom-call(f32[128,128]{1,0:T(8,128)S(1)} %copy.31), custom_call_target="Cholesky" | custom-call | tf_op jit(solution)/shard_map/jit(cholesky)/cholesky | solution.py:56
  106.9 9.8 %custom-call.13 = f32[1,128,128]{1,2,0:T(8,128)S(1)} custom-call(f32[1,128,128]{2,1,0:T(8,128)S(1)} %get-tuple-element.103), custom_call_target="InvertDiagBlocksLowerTriangular" | custom-call | tf_op jit(solution)/shard_map/jit(cholesky)/cholesky | solution.py:56
  119.1 11.7 %cholesky.147 = f32[128,128]{1,0:T(8,128)S(1)} custom-call(f32[128,128]{1,0:T(8,128)S(1)} %copy.33), custom_call_target="Cholesky" | custom-call | tf_op jit(solution)/shard_map/jit(cholesky)/cholesky | solution.py:56
  133.7 4.1 %while.4 = (s32[]{:T(128)}, f32[256,256]{1,0:T(8,128)S(1)}, s32[2,2]{1,0:T(2,128)S(1)}, f32[2,128,128]{2,1,0:T(8,128)S(1)}, s32[]{:T(128)}) while((s32[]{:T(128)}, f32[256,256]{1,0:T(8,128)S(1)}, s32[2,2]{1,0:T(2,128)S(1)}, f32[2,128,128]{2,1,0:T(8,128)S(1)}, s32[]{:T(128)}) %tuple.88), condition=%wide.while_cond, body=%wide.while_body.sunk | while | flops 2 | bytes 131189 | solution.py:57
  137.9 20.1 %custom-call.14 = f32[2,128,128]{1,2,0:T(8,128)S(1)} custom-call(f32[2,128,128]{2,1,0:T(8,128)S(1)} %get-tuple-element.21), custom_call_target="InvertDiagBlocksLowerTriangular" | custom-call | tf_op jit(solution)/shard_map/jit(_solve_triangular)/triangular_solve | solution.py:57
  161.7 1.8 copy.36
  165.4 11.7 %cholesky.164 = f32[128,128]{1,0:T(8,128)S(1)} custom-call(f32[128,128]{1,0:T(8,128)S(1)} %cholesky.197), custom_call_target="Cholesky" | custom-call | tf_op jit(solution)/shard_map/jit(cholesky)/cholesky | solution.py:60
  177.9 9.8 %custom-call.15 = f32[1,128,128]{1,2,0:T(8,128)S(1)} custom-call(f32[1,128,128]{2,1,0:T(8,128)S(1)} %get-tuple-element.99), custom_call_target="InvertDiagBlocksLowerTriangular" | custom-call | tf_op jit(solution)/shard_map/jit(cholesky)/cholesky | solution.py:60
  189.9 11.7 %cholesky.181 = f32[128,128]{1,0:T(8,128)S(1)} custom-call(f32[128,128]{1,0:T(8,128)S(1)} %convolution_subtract_fusion.2), custom_call_target="Cholesky" | custom-call | tf_op jit(solution)/shard_map/jit(cholesky)/cholesky | solution.py:60
  204.6 4.1 %while.5 = (s32[]{:T(128)}, f32[256,256]{1,0:T(8,128)S(1)}, s32[2,2]{1,0:T(2,128)S(1)}, f32[2,128,128]{2,1,0:T(8,128)S(1)}, s32[]{:T(128)}) while((s32[]{:T(128)}, f32[256,256]{1,0:T(8,128)S(1)}, s32[2,2]{1,0:T(2,128)S(1)}, f32[2,128,128]{2,1,0:T(8,128)S(1)}, s32[]{:T(128)}) %tuple.98), condition=%wide.while_cond.clone, body=%wide.while_body.clone.sunk | while | flops 2 | bytes 131189 | solution.py:61
  208.7 19.7 %custom-call.16 = f32[2,128,128]{1,2,0:T(8,128)S(1)} custom-call(f32[2,128,128]{2,1,0:T(8,128)S(1)} %get-tuple-element.22), custom_call_target="InvertDiagBlocksLowerTriangular" | custom-call | tf_op jit(solution)/shard_map/jit(_solve_triangular)/triangular_solve | solution.py:61
  237.4 1.4 collective-permute-start.5
  242.9 1.4 collective-permute-start.1
  253.0 1.9 collective-permute-start.32
  254.9 1.9 collective-permute-start.31
  256.8 1.9 collective-permute-start.30
  258.7 1.9 collective-permute-start.29
  267.3 1.6 add_add_fusion
  273.7 45.1 %all-gather.5.cloned.1.call-done = f32[4864,256]{1,0:T(8,128)} async-done(((f32[152,256]{1,0:T(8,128)}), f32[4864,256]{1,0:T(8,128)}) %all-gather.5.cloned.1.call-update) | async-done | bytes 4980752 | tf_op jit(solution)/shard_map/all_gather | solution.py:72
  320.0 2.6 fusion.58
  322.7 2.5 fusion.3
  325.2 4.4 %fusion.18 = f32[10,256,256]{2,1,0:T(8,128)S(1)} fusion(f32[10,256,256]{1,2,0:T(8,128)S(1)} %fusion.3, f32[384,256]{1,0:T(8,128)S(1)} %bitcast.170, f32[384,256]{1,0:T(8,128)S(1)} %bitcast.173), kind=kOutput, calls=%fused_computation.38 | convolution fusion | flops 2013331456 | bytes 6029312 | tf_op jit(solution)/shard_map/nab,cb->nac/dot_general | solution.py:89
  329.6 2.7 fusion.9
  332.4 2.5 select_select_fusion
  335.2 3.1 copy.47
  338.2 2.3 select_select_fusion.1
  340.5 3.1 copy.43
  343.7 12.6 %select_bitcast_fusion = f32[8,1,256,2,1,256]{5,2,3,0,4,1:T(8,128)} fusion(f32[8,256,256]{1,2,0:T(8,128)S(1)} %copy-done.3, f32[8,256,256]{1,2,0:T(8,128)} %get-tuple-element.54, f32[8,256,256]{2,1,0:T(8,128)} %copy.47, f32[8,256,256]{2,1,0:T(8,128)} %copy.43, pred[8]{0:T(512)(128)(4,1)S(1)} %get-tuple-element.110, pred[2]{0:T(512)(128)(4,1)S(1)} %get-tuple-element.112, ...), kind=kOutput, calls=%fused_computation.9 | convolution fusion | flops 6447955968 | bytes 17825804 | tf_op jit(solution)/shard_map/dot_general | solution.py:100
  356.3 8.5 %copy.50 = f32[8,1,256,2,1,256]{5,4,3,2,1,0:T(1,128)} copy(f32[8,1,256,2,1,256]{5,2,3,0,4,1:T(8,128)} %select_bitcast_fusion) | data formatting | bytes 8388608 | tf_op jit(solution)/shard_map/reshape | solution.py:108
  (218 shorter events, 71.4 us)
Async XLA Ops:
  6.5 264.3 %all-gather.7.cloned.1.call-start = ((), (), s32[]{:S(2)}) async-start(), calls=%async_computation.1 | async-start | bytes 1179648 | tf_op jit(solution)/shard_map/all_gather | solution.py:37
  9.2 18.5 %copy-start.1 = (f32[8,1,256,2,1,256]{5,2,3,0,4,1:T(8,128)}, f32[8,1,256,2,1,256]{5,2,3,0,4,1:T(8,128)S(1)}, u32[]{:S(2)}) copy-start(f32[8,1,256,2,1,256]{5,2,3,0,4,1:T(8,128)S(1)} %copy.66) | copy-start | bytes 12582916
  9.3 66.5 %collective-permute-start.21 = (f32[256,256]{1,0:T(8,128)S(1)}, f32[256,256]{1,0:T(8,128)}, u32[]{:S(2)}, u32[]{:S(2)}) collective-permute-start(f32[256,256]{1,0:T(8,128)S(1)} %slice_bitcast_fusion.6), channel_id=1, source_target_pairs={{0,224},{32,0},{1,225},{33,1},{2,226},{34,2},{3,227},{35,3},{4,228... | collective-permute-start | bytes 786440 | tf_op jit(solution)/shard_map/ppermute | solution.py:46
  17.6 53.4 %collective-permute-start.20 = (f32[256,256]{1,0:T(8,128)S(1)}, f32[256,256]{1,0:T(8,128)}, u32[]{:S(2)}, u32[]{:S(2)}) collective-permute-start(f32[256,256]{1,0:T(8,128)S(1)} %slice_bitcast_fusion.6), channel_id=1, source_target_pairs={{0,192},{32,224},{1,193},{33,225},{2,194},{34,226},{3,195},{35,227... | collective-permute-start | bytes 786440 | tf_op jit(solution)/shard_map/ppermute | solution.py:46
  20.7 47.4 %collective-permute-start.19 = (f32[256,256]{1,0:T(8,128)S(1)}, f32[256,256]{1,0:T(8,128)}, u32[]{:S(2)}, u32[]{:S(2)}) collective-permute-start(f32[256,256]{1,0:T(8,128)S(1)} %slice_bitcast_fusion.6), channel_id=1, source_target_pairs={{0,160},{32,192},{1,161},{33,193},{2,162},{34,194},{3,163},{35,195... | collective-permute-start | bytes 786440 | tf_op jit(solution)/shard_map/ppermute | solution.py:46
  22.6 14.2 %collective-permute-start.16 = (f32[256,256]{1,0:T(8,128)S(1)}, f32[256,256]{1,0:T(8,128)}, u32[]{:S(2)}, u32[]{:S(2)}) collective-permute-start(f32[256,256]{1,0:T(8,128)S(1)} %slice_bitcast_fusion.6), channel_id=1, source_target_pairs={{0,64},{32,96},{1,65},{33,97},{2,66},{34,98},{3,67},{35,99},{4,68}... | collective-permute-start | bytes 786440 | tf_op jit(solution)/shard_map/ppermute | solution.py:46
  24.6 10.0 %collective-permute-start.15 = (f32[256,256]{1,0:T(8,128)S(1)}, f32[256,256]{1,0:T(8,128)}, u32[]{:S(2)}, u32[]{:S(2)}) collective-permute-start(f32[256,256]{1,0:T(8,128)S(1)} %slice_bitcast_fusion.6), channel_id=1, source_target_pairs={{0,32},{32,64},{1,33},{33,65},{2,34},{34,66},{3,35},{35,67},{4,36}... | collective-permute-start | bytes 786440 | tf_op jit(solution)/shard_map/ppermute | solution.py:46
  34.6 5.8 %collective-permute-start.17 = (f32[256,256]{1,0:T(8,128)S(1)}, f32[256,256]{1,0:T(8,128)S(1)}, u32[]{:S(2)}, u32[]{:S(2)}) collective-permute-start(f32[256,256]{1,0:T(8,128)S(1)} %slice_bitcast_fusion.6), channel_id=1, source_target_pairs={{0,96},{32,128},{1,97},{33,129},{2,98},{34,130},{3,99},{35,131},{4... | collective-permute-start | bytes 786440 | tf_op jit(solution)/shard_map/ppermute | solution.py:46
  36.9 9.1 %collective-permute-start.18 = (f32[256,256]{1,0:T(8,128)S(1)}, f32[256,256]{1,0:T(8,128)S(1)}, u32[]{:S(2)}, u32[]{:S(2)}) collective-permute-start(f32[256,256]{1,0:T(8,128)S(1)} %slice_bitcast_fusion.6), channel_id=1, source_target_pairs={{0,128},{32,160},{1,129},{33,161},{2,130},{34,162},{3,131},{35,163... | collective-permute-start | bytes 786440 | tf_op jit(solution)/shard_map/ppermute | solution.py:46
  40.4 43.9 %collective-permute-start.38 = (f32[128,256]{0,1:T(8,128)}, f32[128,256]{0,1:T(8,128)}, u32[]{:S(2)}, u32[]{:S(2)}) collective-permute-start(f32[128,256]{0,1:T(8,128)} %get-tuple-element.78), channel_id=1, source_target_pairs={{0,224},{32,64},{1,225},{33,65},{2,226},{34,66},{3,227},{35,67},{4... | collective-permute-start | bytes 393224 | tf_op jit(solution)/shard_map/ppermute | solution.py:16
  46.0 40.2 %collective-permute-start.40 = (f32[128,256]{0,1:T(8,128)}, f32[128,256]{0,1:T(8,128)}, u32[]{:S(2)}, u32[]{:S(2)}) collective-permute-start(f32[128,256]{0,1:T(8,128)} %get-tuple-element.79), channel_id=1, source_target_pairs={{0,160},{32,128},{1,161},{33,129},{2,162},{34,130},{3,163},{35,131... | collective-permute-start | bytes 393224 | tf_op jit(solution)/shard_map/ppermute | solution.py:16
  68.1 20.1 %collective-permute-start.39 = (f32[128,256]{0,1:T(8,128)}, f32[128,256]{0,1:T(8,128)}, u32[]{:S(2)}, u32[]{:S(2)}) collective-permute-start(f32[128,256]{0,1:T(8,128)} %get-tuple-element.80), channel_id=1, source_target_pairs={{0,192},{32,96},{1,193},{33,97},{2,194},{34,98},{3,195},{35,99},{4... | collective-permute-start | bytes 393224 | tf_op jit(solution)/shard_map/ppermute | solution.py:16
  71.0 158.6 %collective-permute-start = (f32[128,256]{1,0:T(8,128)}, f32[128,256]{1,0:T(8,128)}, u32[]{:S(2)}, u32[]{:S(2)}) collective-permute-start(f32[128,256]{1,0:T(8,128)} %get-tuple-element.57), channel_id=1, source_target_pairs={{0,2},{1,3},{32,34},{33,35},{64,66},{65,67},{96,98},{97,99},{128,1... | collective-permute-start | bytes 393224 | tf_op jit(solution)/shard_map/ppermute | solution.py:16
  80.1 11.9 %collective-permute-start.22 = (f32[256,256]{1,0:T(8,128)}, f32[256,256]{1,0:T(8,128)S(1)}, u32[]{:S(2)}, u32[]{:S(2)}) collective-permute-start(f32[256,256]{1,0:T(8,128)} %get-tuple-element.43), channel_id=1, source_target_pairs={{0,1},{1,0},{32,33},{33,32},{64,65},{65,64},{96,97},{97,96},{128,1... | collective-permute-start | bytes 786440 | tf_op jit(solution)/shard_map/ppermute | solution.py:52
  84.3 146.6 %collective-permute-start.14 = (f32[128,256]{1,0:T(8,128)}, f32[128,256]{1,0:T(8,128)}, u32[]{:S(2)}, u32[]{:S(2)}) collective-permute-start(f32[128,256]{1,0:T(8,128)} %get-tuple-element.58), channel_id=1, source_target_pairs={{0,30},{1,31},{32,62},{33,63},{64,94},{65,95},{96,126},{97,127},{1... | collective-permute-start | bytes 393224 | tf_op jit(solution)/shard_map/ppermute | solution.py:16
  86.3 146.0 %collective-permute-start.13 = (f32[128,256]{1,0:T(8,128)}, f32[128,256]{1,0:T(8,128)}, u32[]{:S(2)}, u32[]{:S(2)}) collective-permute-start(f32[128,256]{1,0:T(8,128)} %get-tuple-element.59), channel_id=1, source_target_pairs={{0,28},{1,29},{32,60},{33,61},{64,92},{65,93},{96,124},{97,125},{1... | collective-permute-start | bytes 393224 | tf_op jit(solution)/shard_map/ppermute | solution.py:16
  88.2 145.3 %collective-permute-start.12 = (f32[128,256]{1,0:T(8,128)}, f32[128,256]{1,0:T(8,128)}, u32[]{:S(2)}, u32[]{:S(2)}) collective-permute-start(f32[128,256]{1,0:T(8,128)} %get-tuple-element.60), channel_id=1, source_target_pairs={{0,26},{1,27},{32,58},{33,59},{64,90},{65,91},{96,122},{97,123},{1... | collective-permute-start | bytes 393224 | tf_op jit(solution)/shard_map/ppermute | solution.py:16
  92.0 226.9 %all-gather.5.cloned.1.call-start = ((), (), s32[]{:S(2)}) async-start(), calls=%async_computation | async-start | bytes 5136384 | tf_op jit(solution)/shard_map/all_gather | solution.py:72
  92.0 142.8 %collective-permute-start.11 = (f32[128,256]{1,0:T(8,128)}, f32[128,256]{1,0:T(8,128)}, u32[]{:S(2)}, u32[]{:S(2)}) collective-permute-start(f32[128,256]{1,0:T(8,128)} %get-tuple-element.61), channel_id=1, source_target_pairs={{0,24},{1,25},{32,56},{33,57},{64,88},{65,89},{96,120},{97,121},{1... | collective-permute-start | bytes 393224 | tf_op jit(solution)/shard_map/ppermute | solution.py:16
  229.6 7.8 %collective-permute-start.10 = (f32[128,256]{1,0:T(8,128)}, f32[128,256]{1,0:T(8,128)S(1)}, u32[]{:S(2)}, u32[]{:S(2)}) collective-permute-start(f32[128,256]{1,0:T(8,128)} %get-tuple-element.62), channel_id=1, source_target_pairs={{0,22},{1,23},{32,54},{33,55},{64,86},{65,87},{96,118},{97,119},{1... | collective-permute-start | bytes 393224 | tf_op jit(solution)/shard_map/ppermute | solution.py:16
  230.9 7.9 %collective-permute-start.9 = (f32[128,256]{1,0:T(8,128)}, f32[128,256]{1,0:T(8,128)S(1)}, u32[]{:S(2)}, u32[]{:S(2)}) collective-permute-start(f32[128,256]{1,0:T(8,128)} %get-tuple-element.63), channel_id=1, source_target_pairs={{0,20},{1,21},{32,52},{33,53},{64,84},{65,85},{96,116},{97,117},{1... | collective-permute-start | bytes 393224 | tf_op jit(solution)/shard_map/ppermute | solution.py:16
  232.2 7.9 %collective-permute-start.8 = (f32[128,256]{1,0:T(8,128)}, f32[128,256]{1,0:T(8,128)S(1)}, u32[]{:S(2)}, u32[]{:S(2)}) collective-permute-start(f32[128,256]{1,0:T(8,128)} %get-tuple-element.64), channel_id=1, source_target_pairs={{0,18},{1,19},{32,50},{33,51},{64,82},{65,83},{96,114},{97,115},{1... | collective-permute-start | bytes 393224 | tf_op jit(solution)/shard_map/ppermute | solution.py:16
  233.5 8.0 %collective-permute-start.7 = (f32[128,256]{1,0:T(8,128)}, f32[128,256]{1,0:T(8,128)S(1)}, u32[]{:S(2)}, u32[]{:S(2)}) collective-permute-start(f32[128,256]{1,0:T(8,128)} %get-tuple-element.65), channel_id=1, source_target_pairs={{0,16},{1,17},{32,48},{33,49},{64,80},{65,81},{96,112},{97,113},{1... | collective-permute-start | bytes 393224 | tf_op jit(solution)/shard_map/ppermute | solution.py:16
  234.9 8.0 %collective-permute-start.6 = (f32[128,256]{1,0:T(8,128)}, f32[128,256]{1,0:T(8,128)S(1)}, u32[]{:S(2)}, u32[]{:S(2)}) collective-permute-start(f32[128,256]{1,0:T(8,128)} %get-tuple-element.66), channel_id=1, source_target_pairs={{0,14},{1,15},{32,46},{33,47},{64,78},{65,79},{96,110},{97,111},{1... | collective-permute-start | bytes 393224 | tf_op jit(solution)/shard_map/ppermute | solution.py:16
  237.4 33.2 %copy-start.7 = (f32[256,256]{1,0:T(8,128)S(1)}, f32[256,256]{1,0:T(8,128)}, u32[]{:S(2)}) copy-start(f32[256,256]{1,0:T(8,128)} %get-tuple-element.42) | copy-start | bytes 786436
  237.4 7.6 %collective-permute-start.5 = (f32[128,256]{1,0:T(8,128)}, f32[128,256]{1,0:T(8,128)S(1)}, u32[]{:S(2)}, u32[]{:S(2)}) collective-permute-start(f32[128,256]{1,0:T(8,128)} %get-tuple-element.67), channel_id=1, source_target_pairs={{0,12},{1,13},{32,44},{33,45},{64,76},{65,77},{96,108},{97,109},{1... | collective-permute-start | bytes 393224 | tf_op jit(solution)/shard_map/ppermute | solution.py:16
  238.9 7.5 %collective-permute-start.4 = (f32[128,256]{1,0:T(8,128)}, f32[128,256]{1,0:T(8,128)S(1)}, u32[]{:S(2)}, u32[]{:S(2)}) collective-permute-start(f32[128,256]{1,0:T(8,128)} %get-tuple-element.68), channel_id=1, source_target_pairs={{0,10},{1,11},{32,42},{33,43},{64,74},{65,75},{96,106},{97,107},{1... | collective-permute-start | bytes 393224 | tf_op jit(solution)/shard_map/ppermute | solution.py:16
  240.2 7.4 %collective-permute-start.3 = (f32[128,256]{1,0:T(8,128)}, f32[128,256]{1,0:T(8,128)S(1)}, u32[]{:S(2)}, u32[]{:S(2)}) collective-permute-start(f32[128,256]{1,0:T(8,128)} %get-tuple-element.69), channel_id=1, source_target_pairs={{0,8},{1,9},{32,40},{33,41},{64,72},{65,73},{96,104},{97,105},{128... | collective-permute-start | bytes 393224 | tf_op jit(solution)/shard_map/ppermute | solution.py:16
  241.5 7.4 %collective-permute-start.2 = (f32[128,256]{1,0:T(8,128)}, f32[128,256]{1,0:T(8,128)S(1)}, u32[]{:S(2)}, u32[]{:S(2)}) collective-permute-start(f32[128,256]{1,0:T(8,128)} %get-tuple-element.70), channel_id=1, source_target_pairs={{0,6},{1,7},{32,38},{33,39},{64,70},{65,71},{96,102},{97,103},{128... | collective-permute-start | bytes 393224 | tf_op jit(solution)/shard_map/ppermute | solution.py:16
  242.8 27.9 %copy-start.8 = (f32[256,256]{1,0:T(8,128)S(1)}, f32[256,256]{1,0:T(8,128)}, u32[]{:S(2)}) copy-start(f32[256,256]{1,0:T(8,128)} %get-tuple-element.40) | copy-start | bytes 786436
  242.9 7.4 %collective-permute-start.1 = (f32[128,256]{1,0:T(8,128)S(1)}, f32[128,256]{1,0:T(8,128)S(1)}, u32[]{:S(2)}, u32[]{:S(2)}) collective-permute-start(f32[128,256]{1,0:T(8,128)S(1)} %get-tuple-element.71), channel_id=1, source_target_pairs={{0,4},{1,5},{32,36},{33,37},{64,68},{65,69},{96,100},{97,101},{128... | collective-permute-start | bytes 393224 | tf_op jit(solution)/shard_map/ppermute | solution.py:16
  245.0 6.6 %collective-permute-start.23 = (f32[24,256]{1,0:T(8,128)S(1)}, f32[24,256]{1,0:T(8,128)S(1)}, u32[]{:S(2)}, u32[]{:S(2)}) collective-permute-start(f32[24,256]{1,0:T(8,128)S(1)} %get-tuple-element.81), channel_id=1, source_target_pairs={{0,2},{1,3},{32,34},{33,35},{64,66},{65,67},{96,98},{97,99},{128,1... | collective-permute-start | bytes 73736 | tf_op jit(solution)/shard_map/ppermute | solution.py:16
  246.3 6.6 %collective-permute-start.37 = (f32[24,256]{1,0:T(8,128)S(1)}, f32[24,256]{1,0:T(8,128)S(1)}, u32[]{:S(2)}, u32[]{:S(2)}) collective-permute-start(f32[24,256]{1,0:T(8,128)S(1)} %get-tuple-element.82), channel_id=1, source_target_pairs={{0,30},{1,31},{32,62},{33,63},{64,94},{65,95},{96,126},{97,127},{1... | collective-permute-start | bytes 73736 | tf_op jit(solution)/shard_map/ppermute | solution.py:16
  247.6 18.3 %copy-start.20 = (f32[128,256]{1,0:T(8,128)}, f32[128,256]{1,0:T(8,128)S(1)}, u32[]{:S(2)}) copy-start(f32[128,256]{1,0:T(8,128)S(1)} %collective-permute-done.3) | copy-start | bytes 393220
  247.6 7.2 %collective-permute-start.36 = (f32[24,256]{1,0:T(8,128)S(1)}, f32[24,256]{1,0:T(8,128)S(1)}, u32[]{:S(2)}, u32[]{:S(2)}) collective-permute-start(f32[24,256]{1,0:T(8,128)S(1)} %get-tuple-element.83), channel_id=1, source_target_pairs={{0,28},{1,29},{32,60},{33,61},{64,92},{65,93},{96,124},{97,125},{1... | collective-permute-start | bytes 73736 | tf_op jit(solution)/shard_map/ppermute | solution.py:16
  249.0 7.8 %collective-permute-start.35 = (f32[24,256]{1,0:T(8,128)S(1)}, f32[24,256]{1,0:T(8,128)S(1)}, u32[]{:S(2)}, u32[]{:S(2)}) collective-permute-start(f32[24,256]{1,0:T(8,128)S(1)} %get-tuple-element.84), channel_id=1, source_target_pairs={{0,26},{1,27},{32,58},{33,59},{64,90},{65,91},{96,122},{97,123},{1... | collective-permute-start | bytes 73736 | tf_op jit(solution)/shard_map/ppermute | solution.py:16
  250.3 8.3 %collective-permute-start.34 = (f32[24,256]{1,0:T(8,128)S(1)}, f32[24,256]{1,0:T(8,128)S(1)}, u32[]{:S(2)}, u32[]{:S(2)}) collective-permute-start(f32[24,256]{1,0:T(8,128)S(1)} %get-tuple-element.85), channel_id=1, source_target_pairs={{0,24},{1,25},{32,56},{33,57},{64,88},{65,89},{96,120},{97,121},{1... | collective-permute-start | bytes 73736 | tf_op jit(solution)/shard_map/ppermute | solution.py:16
  251.7 8.9 %collective-permute-start.33 = (f32[24,256]{1,0:T(8,128)}, f32[24,256]{1,0:T(8,128)S(1)}, u32[]{:S(2)}, u32[]{:S(2)}) collective-permute-start(f32[24,256]{1,0:T(8,128)} %get-tuple-element.86), channel_id=1, source_target_pairs={{0,22},{1,23},{32,54},{33,55},{64,86},{65,87},{96,118},{97,119},{1... | collective-permute-start | bytes 73736 | tf_op jit(solution)/shard_map/ppermute | solution.py:16
  253.0 9.0 %collective-permute-start.32 = (f32[24,256]{1,0:T(8,128)}, f32[24,256]{1,0:T(8,128)}, u32[]{:S(2)}, u32[]{:S(2)}) collective-permute-start(f32[24,256]{1,0:T(8,128)} %get-tuple-element.87), channel_id=1, source_target_pairs={{0,20},{1,21},{32,52},{33,53},{64,84},{65,85},{96,116},{97,117},{1... | collective-permute-start | bytes 73736 | tf_op jit(solution)/shard_map/ppermute | solution.py:16
  254.9 8.4 %collective-permute-start.31 = (f32[24,256]{1,0:T(8,128)}, f32[24,256]{1,0:T(8,128)}, u32[]{:S(2)}, u32[]{:S(2)}) collective-permute-start(f32[24,256]{1,0:T(8,128)} %get-tuple-element.88), channel_id=1, source_target_pairs={{0,18},{1,19},{32,50},{33,51},{64,82},{65,83},{96,114},{97,115},{1... | collective-permute-start | bytes 73736 | tf_op jit(solution)/shard_map/ppermute | solution.py:16
  256.8 7.9 %collective-permute-start.30 = (f32[24,256]{1,0:T(8,128)}, f32[24,256]{1,0:T(8,128)}, u32[]{:S(2)}, u32[]{:S(2)}) collective-permute-start(f32[24,256]{1,0:T(8,128)} %get-tuple-element.89), channel_id=1, source_target_pairs={{0,16},{1,17},{32,48},{33,49},{64,80},{65,81},{96,112},{97,113},{1... | collective-permute-start | bytes 73736 | tf_op jit(solution)/shard_map/ppermute | solution.py:16
  258.7 7.3 %collective-permute-start.29 = (f32[24,256]{1,0:T(8,128)}, f32[24,256]{1,0:T(8,128)}, u32[]{:S(2)}, u32[]{:S(2)}) collective-permute-start(f32[24,256]{1,0:T(8,128)} %get-tuple-element.90), channel_id=1, source_target_pairs={{0,14},{1,15},{32,46},{33,47},{64,78},{65,79},{96,110},{97,111},{1... | collective-permute-start | bytes 73736 | tf_op jit(solution)/shard_map/ppermute | solution.py:16
  260.6 8.3 %collective-permute-start.28 = (f32[24,256]{1,0:T(8,128)}, f32[24,256]{1,0:T(8,128)S(1)}, u32[]{:S(2)}, u32[]{:S(2)}) collective-permute-start(f32[24,256]{1,0:T(8,128)} %get-tuple-element.91), channel_id=1, source_target_pairs={{0,12},{1,13},{32,44},{33,45},{64,76},{65,77},{96,108},{97,109},{1... | collective-permute-start | bytes 73736 | tf_op jit(solution)/shard_map/ppermute | solution.py:16
  262.0 6.9 %collective-permute-start.27 = (f32[24,256]{1,0:T(8,128)}, f32[24,256]{1,0:T(8,128)S(1)}, u32[]{:S(2)}, u32[]{:S(2)}) collective-permute-start(f32[24,256]{1,0:T(8,128)} %get-tuple-element.92), channel_id=1, source_target_pairs={{0,10},{1,11},{32,42},{33,43},{64,74},{65,75},{96,106},{97,107},{1... | collective-permute-start | bytes 73736 | tf_op jit(solution)/shard_map/ppermute | solution.py:16
  263.3 5.6 %collective-permute-start.26 = (f32[24,256]{1,0:T(8,128)}, f32[24,256]{1,0:T(8,128)S(1)}, u32[]{:S(2)}, u32[]{:S(2)}) collective-permute-start(f32[24,256]{1,0:T(8,128)} %get-tuple-element.93), channel_id=1, source_target_pairs={{0,8},{1,9},{32,40},{33,41},{64,72},{65,73},{96,104},{97,105},{128... | collective-permute-start | bytes 73736 | tf_op jit(solution)/shard_map/ppermute | solution.py:16
  264.6 4.3 %collective-permute-start.25 = (f32[24,256]{1,0:T(8,128)}, f32[24,256]{1,0:T(8,128)S(1)}, u32[]{:S(2)}, u32[]{:S(2)}) collective-permute-start(f32[24,256]{1,0:T(8,128)} %get-tuple-element.94), channel_id=1, source_target_pairs={{0,6},{1,7},{32,38},{33,39},{64,70},{65,71},{96,102},{97,103},{128... | collective-permute-start | bytes 73736 | tf_op jit(solution)/shard_map/ppermute | solution.py:16
  266.0 3.0 collective-permute-start.24
  325.2 13.1 %copy-start = (f32[10,256,256]{1,2,0:T(8,128)}, f32[10,256,256]{1,2,0:T(8,128)S(1)}, u32[]{:S(2)}) copy-start(f32[10,256,256]{1,2,0:T(8,128)S(1)} %fusion.3) | copy-start | bytes 7864324
  (31 other events, 148.4 us)
Sparse Core Ops, SparseCore 0:
  92.1 27.9 all-gather.6
  270.6 48.1 all-gather.4
